TPU v7x, 128 devices: a whole 4x4x4 slice. The times are simulated.
128 devices in a mesh: dp: 16 (over z, y), vocab: 8 (over x, core).
Axes of the slice: x: 4, y: 4, z: 4, core: 2. Of those that a mesh axis runs over, the one named last changes fastest.
Arguments:
- hidden: bfloat16 [32, 512, 1024], P('dp'), may hold values from -24 to 24
- norm_gain: float32 [1024], replicated, may hold values from 0.5 to 1.5
- head: bfloat16 [1024, 32000], P('dp', 'vocab'), may hold values from -4 to 4
- targets: int32 [32, 512], P('dp'), may hold values from 0 to 31999
- lengths: int32 [32], P('dp'), may hold values from 1 to 512, 9216 in all
- groups: int32 [32, 1], P('dp'), may hold values from 0 to 3
- baseline: float32 [4], replicated, may hold values from -2 to 0
Outputs:
- logprob: float32 [32, 512], P('dp')
- entropy: float32 [32, 512], P('dp')
- group_shift: float32 [2, 4], replicated
Inputs may be any that keep to these rules, and one draw needn't show every extreme that they name: `groups`: every group holds at least one sequence.
All inputs are finite; a program needn't handle non-finite values. No bound on the sum of `lengths` on one device may be relied on, other than what follows from the above.
Results may differ from a plain program's by a relative error of at most 0.00045.
The roundings to bfloat16 on the way count: a program that leaves them out, or rounds other values in their place, can miss the bound.
Values may be sent and summed in bfloat16 or wider, within the bound.
No kernel may reach another device: no remote copies, remote signals or barrier semaphores. Data moves between devices by JAX's collectives and lax.ppermute only.
A program may use at most 64 MiB of HBM per device.

v0:
```python
import jax
import jax.numpy as jnp
from jax import lax
from jax.sharding import PartitionSpec as P


def per_device(hidden, norm_gain, head, targets, lengths, groups, baseline):
    seq_count, slot_count, width = hidden.shape
    total_rows = seq_count * slot_count
    block = min(512, total_rows)
    weights = lax.all_gather(head, "dp", axis=0, tiled=True)
    vocab_width = weights.shape[1]
    offset = lax.axis_index("vocab") * vocab_width
    flat = hidden.reshape(total_rows, width).astype(jnp.float32)
    square = jnp.mean(flat * flat, axis=-1, keepdims=True)
    normed = (flat * lax.rsqrt(square + 1e-05) * norm_gain[None, :]).astype(jnp.bfloat16)
    positions = jnp.arange(slot_count, dtype=jnp.int32)
    live = (positions[None, :] < lengths[:, None]).reshape(total_rows)
    wanted = targets.reshape(total_rows)
    column = jnp.arange(vocab_width, dtype=jnp.int32) + offset

    def score(rows, picks):
        logits = jnp.dot(rows, weights, preferred_element_type=jnp.float32)
        local_top = jnp.max(logits, axis=-1)
        shifted = logits - local_top[:, None]
        expo = jnp.exp(shifted)
        local_total = jnp.sum(expo, axis=-1)
        local_spread = jnp.sum(expo * shifted, axis=-1)
        chosen = jnp.sum(jnp.where(column[None, :] == picks[:, None], logits, 0.0), axis=-1)
        top = lax.pmax(local_top, "vocab")
        factor = jnp.exp(local_top - top)
        total, spread, target = lax.psum(
            (
                local_total * factor,
                factor * (local_spread + local_total * (local_top - top)),
                chosen,
            ),
            "vocab",
        )
        return (target - top - jnp.log(total), jnp.log(total) - spread / total)

    blocks = (total_rows + block - 1) // block

    def advance(index, carry):
        out_lp, out_ent = carry
        start = index * block
        part_rows = lax.dynamic_slice_in_dim(normed, start, block, 0)
        part_picks = lax.dynamic_slice_in_dim(wanted, start, block, 0)
        block_lp, block_ent = score(part_rows, part_picks)
        out_lp = lax.dynamic_update_slice_in_dim(out_lp, block_lp, start, 0)
        out_ent = lax.dynamic_update_slice_in_dim(out_ent, block_ent, start, 0)
        return (out_lp, out_ent)

    empty = jnp.zeros((normed.shape[0],), jnp.float32)
    logprob, entropy = lax.fori_loop(0, blocks, advance, (empty, empty))
    logprob = jnp.where(live, logprob, 0.0).reshape(seq_count, slot_count)
    entropy = jnp.where(live, entropy, 0.0).reshape(seq_count, slot_count)
    group_count = baseline.shape[0]
    member = (groups[:, 0][:, None] == jnp.arange(group_count, dtype=jnp.int32)[None, :]).astype(
        jnp.float32
    )
    seq_sums = jnp.stack(
        [jnp.sum(logprob, axis=1), jnp.sum(entropy, axis=1), lengths.astype(jnp.float32)], axis=1
    )
    partial_value = jnp.dot(member.T, seq_sums, precision=lax.Precision.HIGHEST)
    group_lp, group_ent, group_cnt = lax.psum(
        (partial_value[:, 0], partial_value[:, 1], partial_value[:, 2]), "dp"
    )
    shift = jnp.stack([group_lp / group_cnt - baseline, group_ent / group_cnt], axis=0)
    return (logprob, entropy, shift)


def solution(mesh):
    placed = (
        P("dp", None, None),
        P(),
        P("dp", "vocab"),
        P("dp", None),
        P("dp"),
        P("dp", None),
        P(),
    )
    return jax.shard_map(
        per_device,
        mesh=mesh,
        in_specs=placed,
        out_specs=(P("dp", None), P("dp", None), P()),
        check_vma=False,
    )
```

profile of v0, /device:TPU:0, one launch (start us, length us, event | category | flops | bytes accessed | tf_op | source)
XLA Modules:
  0.0 203.4 jit_solution(1171368510043875422)
XLA Ops:
  7.2 0.7 all-gather.2.cloned.1.call-update
  7.9 2.1 %multiply_reduce_fusion = f32[2,512]{1,0:T(2,128)S(1)} fusion(bf16[2,512,1024]{2,1,0:T(8,128)(2,1)} %param.9), kind=kLoop, calls=%fused_computation.16 | loop fusion | flops 3144704 | bytes 2101248 | tf_op jit(solution)/shard_map/reduce_sum | solution.py:15
  10.0 0.7 copy.10
  10.7 0.7 iota_compare_fusion
  11.4 0.7 convert_bitcast_fusion
  12.1 2.1 %fusion.7 = bf16[1024,1024]{1,0:T(8,128)(2,1)S(1)} fusion(f32[1024]{0:T(1024)} %param.10, f32[1024]{0:T(1024)S(1)} %bitcast.30, bf16[2,512,1024]{2,1,0:T(8,128)(2,1)} %param.9), kind=kLoop, calls=%fused_computation.15 | loop fusion | flops 4194304 | bytes 4202496 | tf_op jit(solution)/shard_map/convert_element_type | solution.py:16
  14.3 69.3 %all-gather.2.cloned.1.call-done = bf16[1024,4000]{1,0:T(8,128)(2,1)} async-done(((bf16[64,4000]{1,0:T(8,128)(2,1)}), bf16[1024,4000]{1,0:T(8,128)(2,1)}) %all-gather.2.cloned.1.call-update) | async-done | bytes 8192016 | tf_op jit(solution)/shard_map/all_gather | solution.py:11
  83.6 73.4 %while.16 = (s32[]{:T(128)}, f32[1024]{0:T(1024)S(1)}, f32[1024]{0:T(1024)S(1)}, s32[1024]{0:T(1024)S(1)}, bf16[1024,1024]{1,0:T(8,128)(2,1)S(1)}, /*index=5*/bf...) while((s32[]{:T(128)}, f32[1024]{0:T(1024)S(1)}, ...), condition=%wide.region_10.11_spmd.clone, body=%wide.region_1.10_spmd.clone.sunk | while | flops 4210696704 | bytes 25714092 | solution.py:55
  83.6 7.1 %fusion.24 = (f32[512]{0:T(512)S(1)}, f32[512,4000]{0,1:T(8,128)S(1)}) fusion(bf16[1024,4000]{1,0:T(8,128)(2,1)} %get-tuple-element.277, bf16[1024,1024]{1,0:T(8,128)(2,1)S(1)} %get-tuple-element.276, s32[]{:T(128)S(6)} %select_n.33), kind=kOutput, calls=%fused_computation.38.clone.1 | convolution fusion | flops 4196351488 | bytes 17434628 | tf_op jit(solution)/shard_map/while/body/eval_jaxpr/dot_general | solution.py:23
  90.7 0.1 dynamic_slice.23
  90.8 3.2 %fusion.25 = (f32[512]{0:T(512)S(1)}, f32[512]{0:T(512)S(1)}, f32[512]{0:T(512)S(1)}) fusion(f32[512,4000]{0,1:T(8,128)S(1)} %get-tuple-element.238, f32[512]{0:T(512)S(1)} %get-tuple-element.239, s32[512]{0:T(512)S(1)} %dynamic_slice.23, s32[4000]{0:T(1024)S(1)} %iota_add_fusion.2), kind=kLoop, calls=%fused_computation.3.clone.1 | loop fusion | flops 14334464 | bytes 8218240 | tf_op jit(solution)/shard_map/while/body/eval_jaxpr/reduce_sum | solution.py:28
  94.1 14.4 %pmax.13 = f32[512]{0:T(512)S(1)} all-reduce(f32[512]{0:T(512)S(1)} %get-tuple-element.239), channel_id=1, replica_groups=mesh['dp'=16,'vocab'=8] {'vocab'}, use_global_device_ids=true, to_apply=%region_5.5 | all-reduce | flops 512 | bytes 4096 | tf_op jit(solution)/shard_map/while/body/eval_jaxpr/pmax | solution.py:30
  108.5 12.6 %all-reduce.3 = (f32[512]{0:T(512)S(1)}, f32[512]{0:T(512)S(1)}, f32[512]{0:T(512)S(1)}) all-reduce(f32[512]{0:T(512)S(1)} %get-tuple-element.240, f32[512]{0:T(512)S(1)} %get-tuple-element.243, f32[512]{0:T(512)S(1)} %get-tuple-element.244), channel_id=1, replica_groups=mesh['dp'=16,'vocab'=8] {'vocab'}, use_global_device_ids=true, to_apply=%region_3.0 | all-reduce | flops 1536 | bytes 12288 | tf_op jit(solution)/shard_map/while/body/eval_jaxpr/psum | solution.py:32
  121.1 0.1 subtract_dynamic-update-slice_fusion.3
  121.3 7.1 %fusion.24 = (f32[512]{0:T(512)S(1)}, f32[512,4000]{0,1:T(8,128)S(1)}) fusion(bf16[1024,4000]{1,0:T(8,128)(2,1)} %get-tuple-element.277, bf16[1024,1024]{1,0:T(8,128)(2,1)S(1)} %get-tuple-element.276, s32[]{:T(128)S(6)} %select_n.33), kind=kOutput, calls=%fused_computation.38.clone.1 | convolution fusion | flops 4196351488 | bytes 17434628 | tf_op jit(solution)/shard_map/while/body/eval_jaxpr/dot_general | solution.py:23
  128.5 3.2 %fusion.25 = (f32[512]{0:T(512)S(1)}, f32[512]{0:T(512)S(1)}, f32[512]{0:T(512)S(1)}) fusion(f32[512,4000]{0,1:T(8,128)S(1)} %get-tuple-element.238, f32[512]{0:T(512)S(1)} %get-tuple-element.239, s32[512]{0:T(512)S(1)} %dynamic_slice.23, s32[4000]{0:T(1024)S(1)} %iota_add_fusion.2), kind=kLoop, calls=%fused_computation.3.clone.1 | loop fusion | flops 14334464 | bytes 8218240 | tf_op jit(solution)/shard_map/while/body/eval_jaxpr/reduce_sum | solution.py:28
  131.7 12.4 %pmax.13 = f32[512]{0:T(512)S(1)} all-reduce(f32[512]{0:T(512)S(1)} %get-tuple-element.239), channel_id=1, replica_groups=mesh['dp'=16,'vocab'=8] {'vocab'}, use_global_device_ids=true, to_apply=%region_5.5 | all-reduce | flops 512 | bytes 4096 | tf_op jit(solution)/shard_map/while/body/eval_jaxpr/pmax | solution.py:30
  144.2 12.6 %all-reduce.3 = (f32[512]{0:T(512)S(1)}, f32[512]{0:T(512)S(1)}, f32[512]{0:T(512)S(1)}) all-reduce(f32[512]{0:T(512)S(1)} %get-tuple-element.240, f32[512]{0:T(512)S(1)} %get-tuple-element.243, f32[512]{0:T(512)S(1)} %get-tuple-element.244), channel_id=1, replica_groups=mesh['dp'=16,'vocab'=8] {'vocab'}, use_global_device_ids=true, to_apply=%region_3.0 | all-reduce | flops 1536 | bytes 12288 | tf_op jit(solution)/shard_map/while/body/eval_jaxpr/psum | solution.py:32
  156.8 0.1 subtract_dynamic-update-slice_fusion.3
  157.0 0.1 reduce_sum.67
  157.1 0.1 reduce_sum.68
  157.3 0.2 fusion.8
  157.5 38.5 %all-reduce.1 = (f32[4]{0:T(128)S(1)}, f32[4]{0:T(128)S(1)}, f32[4]{0:T(128)S(1)}) all-reduce(f32[4]{0:T(128)S(1)} %get-tuple-element.177, f32[4]{0:T(128)S(1)} %get-tuple-element.178, f32[4]{0:T(128)S(1)} %get-tuple-element.176), channel_id=1, replica_groups=mesh['dp'=16,'vocab'=8] {'dp'}, use_global_device_ids=true, to_apply=%region_15.16 | all-reduce | flops 12 | bytes 96 | tf_op jit(solution)/shard_map/psum | solution.py:66
  195.9 0.6 pad_maximum_fusion
  (24 shorter events, 0.2 us)
Async XLA Ops:
  7.2 76.4 %all-gather.2.cloned.1.call-start = ((), (), s32[]{:S(2)}) async-start(), calls=%async_computation | async-start | bytes 8912896 | tf_op jit(solution)/shard_map/all_gather | solution.py:11
  83.6 73.7 %copy-start.3 = (s32[2,1]{0,1:T(1,128)S(1)}, s32[2,1]{0,1:T(1,128)}, u32[]{:S(2)}) copy-start(s32[2,1]{0,1:T(1,128)} %param.14) | copy-start | bytes 28
  83.6 112.3 %copy-start.2 = (f32[4]{0:T(128)S(1)}, f32[4]{0:T(128)}, u32[]{:S(2)}) copy-start(f32[4]{0:T(128)} %param.15) | copy-start | bytes 52
  157.0 39.5 %copy-start = (f32[2,512]{1,0:T(2,128)}, f32[2,512]{1,0:T(2,128)S(1)}, u32[]{:S(2)}) copy-start(f32[2,512]{1,0:T(2,128)S(1)} %reshape.45) | copy-start | bytes 12292
  157.0 39.5 %copy-start.1 = (f32[2,512]{1,0:T(2,128)}, f32[2,512]{1,0:T(2,128)S(1)}, u32[]{:S(2)}) copy-start(f32[2,512]{1,0:T(2,128)S(1)} %reshape.46) | copy-start | bytes 12292
Sparse Core Ops, SparseCore 0:
  10.1 73.4 all-gather.1
where the time goes:
time: 204 us; the launch traced here: 203 us
  blocking collectives  90.5 us (44%)
  waiting for transfers between devices  70 us (34%)
  matrix products  14.4 us (7%)
  between operations  14.1 us (7%)
  other arithmetic  13.3 us (7%)
    all_gather x1, waiting for transfers between devices, per_device(): weights = lax.all_gather(head, 'dp', axis=0, tiled=True)  69.3 us
    psum x1, blocking collectives, per_device(): lax.psum((partial_value[:, 0], partial_value[:, 1], partial_value[:, 2]),...  38.5 us
    pmax x2, blocking collectives, score(): top = lax.pmax(local_top, 'vocab')  26.8 us
    psum x2, blocking collectives, score(): lax.psum((local_total * factor, factor * (local_spread + local_total * (l...  25.3 us
    dot_general x2, matrix products, score(): logits = jnp.dot(rows, weights, preferred_element_type=jnp.float32)  14.3 us
    reduce_sum x2, other arithmetic, score(): local_spread = jnp.sum(expo * shifted, axis=-1)  6.5 us
  transfers between devices with their start and end apart: 1, of which 1 were waited for; matrix products, arithmetic and copies ran while one was open for 3% of the time, Pallas kernels for 0%

commit v1 on v0

v1 whole, which is shorter than its diff:
```python
import jax
import jax.numpy as jnp
from jax import lax
from jax.sharding import PartitionSpec as P


def per_device(hidden, norm_gain, head, targets, lengths, groups, baseline):
    seq_count, slot_count, width = hidden.shape
    total_rows = seq_count * slot_count
    block = min(512, total_rows)
    weights = lax.all_gather(head, "dp", axis=0, tiled=True)
    vocab_width = weights.shape[1]
    offset = lax.axis_index("vocab") * vocab_width
    flat = hidden.reshape(total_rows, width).astype(jnp.float32)
    square = jnp.mean(flat * flat, axis=-1, keepdims=True)
    normed = (flat * lax.rsqrt(square + 1e-05) * norm_gain[None, :]).astype(jnp.bfloat16)
    positions = jnp.arange(slot_count, dtype=jnp.int32)
    live = (positions[None, :] < lengths[:, None]).reshape(total_rows)
    wanted = targets.reshape(total_rows)
    column = jnp.arange(vocab_width, dtype=jnp.int32) + offset

    def local_stats(rows, picks):
        logits = jnp.dot(rows, weights, preferred_element_type=jnp.float32)
        local_top = jnp.max(logits, axis=-1)
        shifted = logits - local_top[:, None]
        expo = jnp.exp(shifted)
        local_total = jnp.sum(expo, axis=-1)
        local_spread = jnp.sum(expo * shifted, axis=-1)
        chosen = jnp.sum(jnp.where(column[None, :] == picks[:, None], logits, 0.0), axis=-1)
        return jnp.stack([local_top, local_total, local_spread, chosen], axis=0)

    parts = [
        local_stats(normed[start : start + block], wanted[start : start + block])
        for start in range(0, total_rows, block)
    ]
    stats = jnp.concatenate(parts, axis=1)
    gathered = lax.all_gather(stats, "vocab", axis=0)
    tops = gathered[:, 0]
    top = jnp.max(tops, axis=0)
    factor = jnp.exp(tops - top[None, :])
    total = jnp.sum(gathered[:, 1] * factor, axis=0)
    spread = jnp.sum(factor * (gathered[:, 2] + gathered[:, 1] * (tops - top[None, :])), axis=0)
    target = jnp.sum(gathered[:, 3], axis=0)
    log_total = jnp.log(total)
    logprob = target - top - log_total
    entropy = log_total - spread / total
    logprob = jnp.where(live, logprob, 0.0).reshape(seq_count, slot_count)
    entropy = jnp.where(live, entropy, 0.0).reshape(seq_count, slot_count)
    group_count = baseline.shape[0]
    member = (groups[:, 0][:, None] == jnp.arange(group_count, dtype=jnp.int32)[None, :]).astype(
        jnp.float32
    )
    seq_sums = jnp.stack(
        [jnp.sum(logprob, axis=1), jnp.sum(entropy, axis=1), lengths.astype(jnp.float32)], axis=1
    )
    partial_value = jnp.dot(member.T, seq_sums, precision=lax.Precision.HIGHEST)
    group_value = jnp.sum(lax.all_gather(partial_value, "dp", axis=0), axis=0)
    group_lp, group_ent, group_cnt = group_value[:, 0], group_value[:, 1], group_value[:, 2]
    shift = jnp.stack([group_lp / group_cnt - baseline, group_ent / group_cnt], axis=0)
    return (logprob, entropy, shift)


def solution(mesh):
    placed = (
        P("dp", None, None),
        P(),
        P("dp", "vocab"),
        P("dp", None),
        P("dp"),
        P("dp", None),
        P(),
    )
    return jax.shard_map(
        per_device,
        mesh=mesh,
        in_specs=placed,
        out_specs=(P("dp", None), P("dp", None), P()),
        check_vma=False,
    )
```

time: 204 us -> 150 us (0.74)
  blocking collectives: 90.5 us -> 36.1 us
    psum x3 -> x0, blocking collectives: 63.7 us -> none  [the longest x1 38.5 us: per_device(): lax.psum((partial_value[:, 0], partial_value[:, 1], partial_value[:, 2]),...]
    all_gather x0 -> x2, blocking collectives: none -> 36.1 us  [the longest x1 23.1 us: per_device(): group_value = jnp.sum(lax.all_gather(partial_value, 'dp', axis=0), axis=0)]
    pmax x2 -> x0, blocking collectives: 26.8 us -> none  [score(): top = lax.pmax(local_top, 'vocab')]
  transfers between devices with their start and end apart: 1 -> 1, of which waited for: 1 -> 1; matrix products, arithmetic and copies ran while one was open for 3% -> 4% of each run, Pallas kernels for 0% -> 0%
where the time goes in v1:
time: 150 us
  waiting for transfers between devices  70.7 us (47%)
  blocking collectives  36.1 us (24%)
  matrix products  14.6 us (10%)
  between operations  14.2 us (9%)
  other arithmetic  13.3 us (9%)
    all_gather x1, waiting for transfers between devices, per_device(): weights = lax.all_gather(head, 'dp', axis=0, tiled=True)  70 us
    all_gather x1, blocking collectives, per_device(): group_value = jnp.sum(lax.all_gather(partial_value, 'dp', axis=0), axis=0)  23.1 us
    dot_general x2, matrix products, local_stats(): logits = jnp.dot(rows, weights, preferred_element_type=jnp.float32)  14.4 us
    all_gather x1, blocking collectives, per_device(): gathered = lax.all_gather(stats, 'vocab', axis=0)  13.1 us
    reduce_sum x1, other arithmetic, local_stats(): local_total = jnp.sum(expo, axis=-1)  6.58 us
  transfers between devices with their start and end apart: 1, of which 1 were waited for; matrix products, arithmetic and copies ran while one was open for 4% of the time, Pallas kernels for 0%

profile of v1, /device:TPU:0, one launch (start us, length us, event | category | flops | bytes accessed | tf_op | source)
XLA Modules:
  0.0 149.7 jit_solution(2858950695779201116)
XLA Ops:
  7.2 0.0 all-gather.6.cloned.1.call-start
  7.2 0.7 all-gather.6.cloned.1.call-update
  7.9 2.1 %multiply_reduce_fusion = f32[2,512]{1,0:T(2,128)S(1)} fusion(bf16[2,512,1024]{2,1,0:T(8,128)(2,1)} %param.7), kind=kLoop, calls=%fused_computation.11 | loop fusion | flops 3144704 | bytes 2101248 | tf_op jit(solution)/shard_map/reduce_sum | solution.py:15
  10.0 0.7 convert_bitcast_fusion
  10.7 0.8 fusion.29
  11.4 2.1 %fusion.3 = bf16[1024,1024]{1,0:T(8,128)(2,1)S(1)} fusion(f32[1024]{0:T(1024)} %param.8, f32[1024]{0:T(1024)S(1)} %bitcast.56, bf16[2,512,1024]{2,1,0:T(8,128)(2,1)} %param.7), kind=kLoop, calls=%fused_computation.10 | loop fusion | flops 4194304 | bytes 4202496 | tf_op jit(solution)/shard_map/convert_element_type | solution.py:16
  13.6 70.0 %all-gather.6.cloned.1.call-done = bf16[1024,4000]{1,0:T(8,128)(2,1)} async-done(((bf16[64,4000]{1,0:T(8,128)(2,1)}), bf16[1024,4000]{1,0:T(8,128)(2,1)}) %all-gather.6.cloned.1.call-update) | async-done | bytes 8192016 | tf_op jit(solution)/shard_map/all_gather | solution.py:11
  83.6 7.2 %fusion.30 = (f32[512]{0:T(512)S(1)}, f32[512,4000]{0,1:T(8,128)S(1)}) fusion(bf16[1024,4000]{1,0:T(8,128)(2,1)} %all-gather.6.cloned.1.call-done, bf16[1024,1024]{1,0:T(8,128)(2,1)S(1)} %fusion.3), kind=kOutput, calls=%fused_computation.55 | convolution fusion | flops 4196351488 | bytes 17434624 | tf_op jit(solution)/shard_map/dot_general | solution.py:23
  90.8 7.2 %fusion.31 = (f32[512]{0:T(512)S(1)}, f32[512,4000]{0,1:T(8,128)S(1)}) fusion(bf16[1024,4000]{1,0:T(8,128)(2,1)} %all-gather.6.cloned.1.call-done, bf16[1024,1024]{1,0:T(8,128)(2,1)S(1)} %fusion.3), kind=kOutput, calls=%fused_computation.56 | convolution fusion | flops 4196351488 | bytes 17434624 | tf_op jit(solution)/shard_map/dot_general | solution.py:23
  97.9 0.0 copy-start
  98.0 0.0 copy-start.1
  98.0 0.0 copy-start.2
  98.0 6.6 %exponential_reduce_fusion.1 = (f32[512]{0:T(512)S(1)}, f32[512]{0:T(512)S(1)}, f32[512]{0:T(512)S(1)}, f32[512]{0:T(512)S(1)}, f32[512]{0:T(512)S(1)}, /*index=5*/f32[512]{0:T(512)S(1)}) fusion(f32[512,4000]{0,1:T(8,128)S(1)} %get-tuple-element.34, f32[512]{0:T(512)S(1)} %get-tuple-element.33, s32[512]{0:T(512)S(1)} %bitcast.65, s32[4000]{0:T(1024)S(1)} %iota_add_fusion, ...), kind=kLoop, calls=%fused_computation.3 | loop fusion | flops 28668928 | bytes 16420480 | tf_op jit(solution)/shard_map/reduce_sum | solution.py:27
  104.6 13.1 %all-gather.2 = f32[8,4,1024]{2,1,0:T(4,128)S(1)} all-gather(f32[1,4,1024]{2,1,0:T(4,128)S(1)} %maximum_bitcast_fusion), channel_id=2, replica_groups=mesh['dp'=16,'vocab'=8] {'vocab'}, dimensions={0}, use_global_device_ids=true | all-gather | bytes 147456 | tf_op jit(solution)/shard_map/all_gather | solution.py:37
  117.7 0.1 fusion.28
  117.9 0.0 copy-done
  117.9 0.8 fusion.26
  118.7 0.0 copy-done.1
  118.7 0.3 convolution_bitcast_fusion
  118.9 23.1 %all-gather.3 = f32[16,4,3]{2,1,0:T(4,128)S(1)} all-gather(f32[1,4,3]{2,1,0:T(4,128)S(1)} %convolution_bitcast_fusion), channel_id=3, replica_groups=mesh['dp'=16,'vocab'=8] {'dp'}, dimensions={0}, use_global_device_ids=true | all-gather | bytes 816 | tf_op jit(solution)/shard_map/all_gather | solution.py:57
  142.0 0.2 fusion.20
  142.3 0.0 copy-done.2
  142.3 0.6 pad_maximum_fusion
  (10 shorter events, 0.1 us)
Async XLA Ops:
  7.2 76.4 %all-gather.6.cloned.1.call-start = ((), (), s32[]{:S(2)}) async-start(), calls=%async_computation | async-start | bytes 8912896 | tf_op jit(solution)/shard_map/all_gather | solution.py:11
  97.9 19.9 %copy-start = (s32[2]{0:T(128)S(1)}, s32[2]{0:T(128)}, u32[]{:S(2)}) copy-start(s32[2]{0:T(128)} %param.11) | copy-start | bytes 28
  98.0 20.7 %copy-start.1 = (s32[2,1]{0,1:T(1,128)S(1)}, s32[2,1]{0,1:T(1,128)}, u32[]{:S(2)}) copy-start(s32[2,1]{0,1:T(1,128)} %param.12) | copy-start | bytes 28
  98.0 44.3 %copy-start.2 = (f32[4]{0:T(128)S(1)}, f32[4]{0:T(128)}, u32[]{:S(2)}) copy-start(f32[4]{0:T(128)} %param.13) | copy-start | bytes 52
Sparse Core Ops, SparseCore 0:
  10.1 73.4 all-gather.5

commit v2 on v1

--- a/solution.py
+++ b/solution.py
@@ -34,7 +34,9 @@
         for start in range(0, total_rows, block)
     ]
     stats = jnp.concatenate(parts, axis=1)
-    gathered = lax.all_gather(stats, "vocab", axis=0)
+    vocab_count = lax.axis_size("vocab")
+    spread_out = jnp.broadcast_to(stats[None], (vocab_count,) + stats.shape)
+    gathered = lax.all_to_all(spread_out, "vocab", 0, 0, tiled=False)
     tops = gathered[:, 0]
     top = jnp.max(tops, axis=0)
     factor = jnp.exp(tops - top[None, :])
@@ -54,7 +56,9 @@
         [jnp.sum(logprob, axis=1), jnp.sum(entropy, axis=1), lengths.astype(jnp.float32)], axis=1
     )
     partial_value = jnp.dot(member.T, seq_sums, precision=lax.Precision.HIGHEST)
-    group_value = jnp.sum(lax.all_gather(partial_value, "dp", axis=0), axis=0)
+    dp_count = lax.axis_size("dp")
+    partial_out = jnp.broadcast_to(partial_value[None], (dp_count,) + partial_value.shape)
+    group_value = jnp.sum(lax.all_to_all(partial_out, "dp", 0, 0, tiled=False), axis=0)
     group_lp, group_ent, group_cnt = group_value[:, 0], group_value[:, 1], group_value[:, 2]
     shift = jnp.stack([group_lp / group_cnt - baseline, group_ent / group_cnt], axis=0)
     return (logprob, entropy, shift)

time: 150 us -> 137 us (0.913)
  blocking collectives: 36.1 us -> 12.7 us
  waiting for transfers between devices: 70.7 us -> 77.4 us
  starting transfers between devices: 0.04 us -> 4.3 us
    all_gather x2 -> x0, blocking collectives: 36.1 us -> none  [the longest x1 23.1 us: per_device(): group_value = jnp.sum(lax.all_gather(partial_value, 'dp', axis=0), axis=0)]
    all_to_all x0 -> x1, blocking collectives: none -> 12.7 us  [per_device(): lax.all_to_all(partial_out, 'dp', 0, 0, tiled=False)]
    all_to_all x0 -> x1, waiting for transfers between devices: none -> 6.09 us  [per_device(): gathered = lax.all_to_all(spread_out, 'vocab', 0, 0, tiled=False)]
    all_to_all x0 -> x1, starting transfers between devices: none -> 4.26 us  [per_device(): gathered = lax.all_to_all(spread_out, 'vocab', 0, 0, tiled=False)]
  transfers between devices with their start and end apart: 1 -> 2, of which waited for: 1 -> 2; matrix products, arithmetic and copies ran while one was open for 4% -> 4% of each run, Pallas kernels for 0% -> 0%
where the time goes in v2:
time: 137 us
  waiting for transfers between devices  77.4 us (56%)
  matrix products  14.5 us (11%)
  between operations  14.2 us (10%)
  blocking collectives  12.7 us (9%)
  other arithmetic  12.4 us (9%)
  starting transfers between devices  4.3 us (3%)
  local copies, waits for them, and re-layouts  1.47 us (1%)
    all_gather x1, waiting for transfers between devices, per_device(): weights = lax.all_gather(head, 'dp', axis=0, tiled=True)  70.6 us
    dot_general x2, matrix products, local_stats(): logits = jnp.dot(rows, weights, preferred_element_type=jnp.float32)  14.4 us
    all_to_all x1, blocking collectives, per_device(): lax.all_to_all(partial_out, 'dp', 0, 0, tiled=False)  12.7 us
    reduce_sum x1, other arithmetic, local_stats(): local_total = jnp.sum(expo, axis=-1)  6.58 us
    all_to_all x1, waiting for transfers between devices, per_device(): gathered = lax.all_to_all(spread_out, 'vocab', 0, 0, tiled=False)  6.09 us
    all_to_all x1, starting transfers between devices, per_device(): gathered = lax.all_to_all(spread_out, 'vocab', 0, 0, tiled=False)  4.26 us
  transfers between devices with their start and end apart: 2, of which 2 were waited for; matrix products, arithmetic and copies ran while one was open for 4% of the time, Pallas kernels for 0%

profile of v2, /device:TPU:0, one launch (start us, length us, event | category | flops | bytes accessed | tf_op | source)
XLA Modules:
  0.0 137.0 jit_solution(7105504285659255126)
XLA Ops:
  7.2 0.0 all-gather.2.cloned.1.call-start
  7.2 0.7 all-gather.2.cloned.1.call-update
  7.9 2.1 %multiply_reduce_fusion = f32[2,512]{1,0:T(2,128)S(1)} fusion(bf16[2,512,1024]{2,1,0:T(8,128)(2,1)} %param.7), kind=kLoop, calls=%fused_computation.11 | loop fusion | flops 3144704 | bytes 2101248 | tf_op jit(solution)/shard_map/reduce_sum | solution.py:15
  10.0 0.8 fusion.30
  10.8 2.1 %fusion.3 = bf16[1024,1024]{1,0:T(8,128)(2,1)S(1)} fusion(f32[1024]{0:T(1024)} %param.8, f32[1024]{0:T(1024)S(1)} %bitcast.54, bf16[2,512,1024]{2,1,0:T(8,128)(2,1)} %param.7), kind=kLoop, calls=%fused_computation.10 | loop fusion | flops 4194304 | bytes 4202496 | tf_op jit(solution)/shard_map/convert_element_type | solution.py:16
  12.9 70.6 %all-gather.2.cloned.1.call-done = bf16[1024,4000]{1,0:T(8,128)(2,1)} async-done(((bf16[64,4000]{1,0:T(8,128)(2,1)}), bf16[1024,4000]{1,0:T(8,128)(2,1)}) %all-gather.2.cloned.1.call-update) | async-done | bytes 8192016 | tf_op jit(solution)/shard_map/all_gather | solution.py:11
  83.6 7.2 %fusion.31 = (f32[512]{0:T(512)S(1)}, f32[512,4000]{0,1:T(8,128)S(1)}) fusion(bf16[1024,4000]{1,0:T(8,128)(2,1)} %all-gather.2.cloned.1.call-done, bf16[1024,1024]{1,0:T(8,128)(2,1)S(1)} %fusion.3), kind=kOutput, calls=%fused_computation.54 | convolution fusion | flops 4196351488 | bytes 17434624 | tf_op jit(solution)/shard_map/dot_general | solution.py:23
  90.8 7.2 %fusion.32 = (f32[512]{0:T(512)S(1)}, f32[512,4000]{0,1:T(8,128)S(1)}) fusion(bf16[1024,4000]{1,0:T(8,128)(2,1)} %all-gather.2.cloned.1.call-done, bf16[1024,1024]{1,0:T(8,128)(2,1)S(1)} %fusion.3), kind=kOutput, calls=%fused_computation.55 | convolution fusion | flops 4196351488 | bytes 17434624 | tf_op jit(solution)/shard_map/dot_general | solution.py:23
  97.9 0.0 copy-start
  98.0 0.0 copy-start.2
  98.0 0.0 copy-start.1
  98.0 6.6 %exponential_reduce_fusion.1 = (f32[512]{0:T(512)S(1)}, f32[512]{0:T(512)S(1)}, f32[512]{0:T(512)S(1)}, f32[512]{0:T(512)S(1)}, f32[512]{0:T(512)S(1)}, /*index=5*/f32[512]{0:T(512)S(1)}) fusion(f32[512,4000]{0,1:T(8,128)S(1)} %get-tuple-element.32, f32[512]{0:T(512)S(1)} %get-tuple-element.31, s32[512]{0:T(512)S(1)} %bitcast.63, s32[4000]{0:T(1024)S(1)} %iota_add_fusion, ...), kind=kLoop, calls=%fused_computation.3 | loop fusion | flops 28668928 | bytes 16420480 | tf_op jit(solution)/shard_map/reduce_sum | solution.py:27
  104.6 0.7 broadcast_in_dim.14
  105.2 4.3 %all-to-all-start = ((f32[8,4,1024]{2,1,0:T(4,128)}), f32[8,4,1024]{2,1,0:T(4,128)S(1)}, u32[]{:S(2)}, u32[]{:S(2)}) async-start(f32[8,4,1024]{2,1,0:T(4,128)} %broadcast_in_dim.14), calls=%async_computation | async-start | bytes 262144 | tf_op jit(solution)/shard_map/all_to_all | solution.py:39
  109.5 0.0 copy-done
  109.5 6.1 %all-to-all-done = f32[8,4,1024]{2,1,0:T(4,128)S(1)} async-done(((f32[8,4,1024]{2,1,0:T(4,128)}), f32[8,4,1024]{2,1,0:T(4,128)S(1)}, u32[]{:S(2)}, u32[]{:S(2)}) %all-to-all-start) | async-done | bytes 131104 | tf_op jit(solution)/shard_map/all_to_all | solution.py:39
  115.6 0.1 fusion.29
  115.8 0.8 fusion.27
  116.6 0.0 copy-done.2
  116.6 0.2 fusion.13
  116.8 12.7 %all_to_all.10 = f32[16,4,3]{1,2,0:T(4,128)S(1)} all-to-all(f32[16,4,3]{1,2,0:T(4,128)S(1)} %broadcast_in_dim.16), channel_id=1, replica_groups=mesh['dp'=16,'vocab'=8] {'dp'}, dimensions={0} | all-to-all | bytes 1536 | tf_op jit(solution)/shard_map/all_to_all | solution.py:61
  129.6 0.0 copy-done.1
  129.6 0.6 pad_maximum_fusion
  (13 shorter events, 0.2 us)
Async XLA Ops:
  7.2 76.4 %all-gather.2.cloned.1.call-start = ((), (), s32[]{:S(2)}) async-start(), calls=%async_computation.2 | async-start | bytes 8912896 | tf_op jit(solution)/shard_map/all_gather | solution.py:11
  97.9 11.6 %copy-start = (s32[2]{0:T(128)S(1)}, s32[2]{0:T(128)}, u32[]{:S(2)}) copy-start(s32[2]{0:T(128)} %param.11) | copy-start | bytes 28
  98.0 18.7 %copy-start.2 = (s32[2,1]{0,1:T(1,128)S(1)}, s32[2,1]{0,1:T(1,128)}, u32[]{:S(2)}) copy-start(s32[2,1]{0,1:T(1,128)} %param.12) | copy-start | bytes 28
  98.0 31.6 %copy-start.1 = (f32[4]{0:T(128)S(1)}, f32[4]{0:T(128)}, u32[]{:S(2)}) copy-start(f32[4]{0:T(128)} %param.13) | copy-start | bytes 52
  105.2 10.4 %all-to-all-start = ((f32[8,4,1024]{2,1,0:T(4,128)}), f32[8,4,1024]{2,1,0:T(4,128)S(1)}, u32[]{:S(2)}, u32[]{:S(2)}) async-start(f32[8,4,1024]{2,1,0:T(4,128)} %broadcast_in_dim.14), calls=%async_computation | async-start | bytes 262144 | tf_op jit(solution)/shard_map/all_to_all | solution.py:39
Sparse Core Ops, SparseCore 0:
  10.1 73.4 all-gather.1

commit v3 on v2

--- a/solution.py
+++ b/solution.py
@@ -7,7 +7,7 @@
 def per_device(hidden, norm_gain, head, targets, lengths, groups, baseline):
     seq_count, slot_count, width = hidden.shape
     total_rows = seq_count * slot_count
-    block = min(512, total_rows)
+    block = total_rows
     weights = lax.all_gather(head, "dp", axis=0, tiled=True)
     vocab_width = weights.shape[1]
     offset = lax.axis_index("vocab") * vocab_width

time: 137 us -> 144 us (1.051)
  matrix products: 14.5 us -> 19.2 us
  other arithmetic: 12.4 us -> 14.5 us
    dot_general x2 -> x1, matrix products: 14.4 us -> 19 us  [local_stats(): logits = jnp.dot(rows, weights, preferred_element_type=jnp.float32)]
    reduce_sum x1, other arithmetic: 6.58 us -> 8.65 us  [local_stats(): local_total = jnp.sum(expo, axis=-1)]
  transfers between devices with their start and end apart: 2 -> 2, of which waited for: 2 -> 2; matrix products, arithmetic and copies ran while one was open for 4% -> 3% of each run, Pallas kernels for 0% -> 0%
where the time goes in v3:
time: 144 us
  waiting for transfers between devices  77.5 us (54%)
  matrix products  19.2 us (13%)
  other arithmetic  14.5 us (10%)
  between operations  14.1 us (10%)
  blocking collectives  12.7 us (9%)
  starting transfers between devices  4.29 us (3%)
    all_gather x1, waiting for transfers between devices, per_device(): weights = lax.all_gather(head, 'dp', axis=0, tiled=True)  70.7 us
    dot_general x1, matrix products, local_stats(): logits = jnp.dot(rows, weights, preferred_element_type=jnp.float32)  19 us
    all_to_all x1, blocking collectives, per_device(): lax.all_to_all(partial_out, 'dp', 0, 0, tiled=False)  12.7 us
    reduce_sum x1, other arithmetic, local_stats(): local_total = jnp.sum(expo, axis=-1)  8.65 us
    all_to_all x1, waiting for transfers between devices, per_device(): gathered = lax.all_to_all(spread_out, 'vocab', 0, 0, tiled=False)  6.09 us
    all_to_all x1, starting transfers between devices, per_device(): gathered = lax.all_to_all(spread_out, 'vocab', 0, 0, tiled=False)  4.26 us
  transfers between devices with their start and end apart: 2, of which 2 were waited for; matrix products, arithmetic and copies ran while one was open for 3% of the time, Pallas kernels for 0%

profile of v3, /device:TPU:0, one launch (start us, length us, event | category | flops | bytes accessed | tf_op | source)
XLA Modules:
  0.0 143.7 jit_solution(10136714997800871528)
XLA Ops:
  7.2 0.0 all-gather.2.cloned.1.call-start
  7.2 0.7 all-gather.2.cloned.1.call-update
  7.9 2.1 %multiply_reduce_fusion = f32[2,512]{1,0:T(2,128)S(1)} fusion(bf16[2,512,1024]{2,1,0:T(8,128)(2,1)} %param.7), kind=kLoop, calls=%fused_computation.7 | loop fusion | flops 3144704 | bytes 2101248 | tf_op jit(solution)/shard_map/reduce_sum | solution.py:15
  10.0 0.7 copy.27
  10.7 2.1 %fusion.2 = bf16[1024,1024]{1,0:T(8,128)(2,1)S(1)} fusion(f32[1024]{0:T(1024)} %param.8, f32[1024]{0:T(1024)S(1)} %bitcast.55, bf16[2,512,1024]{2,1,0:T(8,128)(2,1)} %param.7), kind=kLoop, calls=%fused_computation.6 | loop fusion | flops 4194304 | bytes 4202496 | tf_op jit(solution)/shard_map/convert_element_type | solution.py:16
  12.9 70.7 %all-gather.2.cloned.1.call-done = bf16[1024,4000]{1,0:T(8,128)(2,1)} async-done(((bf16[64,4000]{1,0:T(8,128)(2,1)}), bf16[1024,4000]{1,0:T(8,128)(2,1)}) %all-gather.2.cloned.1.call-update) | async-done | bytes 8192016 | tf_op jit(solution)/shard_map/all_gather | solution.py:11
  83.6 19.0 %fusion.25 = (f32[1024]{0:T(1024)S(1)}, f32[1024,4000]{0,1:T(8,128)}) fusion(bf16[1024,1024]{1,0:T(8,128)(2,1)S(1)} %fusion.2, bf16[1024,4000]{1,0:T(8,128)(2,1)} %all-gather.2.cloned.1.call-done), kind=kOutput, calls=%fused_computation.45 | convolution fusion | flops 8392702976 | bytes 26677248 | tf_op jit(solution)/shard_map/dot_general | solution.py:23
  102.6 0.0 copy-start
  102.6 0.0 copy-start.2
  102.6 0.0 copy-start.1
  102.6 8.7 %exponential_reduce_fusion = (f32[1024]{0:T(1024)S(1)}, f32[1024]{0:T(1024)S(1)}, f32[1024]{0:T(1024)S(1)}) fusion(f32[1024,4000]{0,1:T(8,128)} %get-tuple-element.24, f32[1024]{0:T(1024)S(1)} %get-tuple-element.23, s32[1024]{0:T(1024)S(1)} %bitcast.50, s32[4000]{0:T(1024)S(1)} %iota_add_fusion), kind=kLoop, calls=%fused_computation.1 | loop fusion | flops 28668928 | bytes 16420480 | tf_op jit(solution)/shard_map/reduce_sum | solution.py:27
  111.3 0.7 broadcast_in_dim.13
  111.9 4.3 %all-to-all-start = ((f32[8,4,1024]{2,1,0:T(4,128)}), f32[8,4,1024]{2,1,0:T(4,128)S(1)}, u32[]{:S(2)}, u32[]{:S(2)}) async-start(f32[8,4,1024]{2,1,0:T(4,128)} %broadcast_in_dim.13), calls=%async_computation | async-start | bytes 262144 | tf_op jit(solution)/shard_map/all_to_all | solution.py:39
  116.2 0.0 copy-done
  116.2 6.1 %all-to-all-done = f32[8,4,1024]{2,1,0:T(4,128)S(1)} async-done(((f32[8,4,1024]{2,1,0:T(4,128)}), f32[8,4,1024]{2,1,0:T(4,128)S(1)}, u32[]{:S(2)}, u32[]{:S(2)}) %all-to-all-start) | async-done | bytes 131104 | tf_op jit(solution)/shard_map/all_to_all | solution.py:39
  122.3 0.1 fusion.24
  122.5 0.8 fusion.22
  123.3 0.0 copy-done.2
  123.3 0.2 fusion.8
  123.5 12.7 %all_to_all.10 = f32[16,4,3]{1,2,0:T(4,128)S(1)} all-to-all(f32[16,4,3]{1,2,0:T(4,128)S(1)} %broadcast_in_dim.16), channel_id=1, replica_groups=mesh['dp'=16,'vocab'=8] {'dp'}, dimensions={0} | all-to-all | bytes 1536 | tf_op jit(solution)/shard_map/all_to_all | solution.py:61
  136.2 0.0 copy-done.1
  136.2 0.6 pad_maximum_fusion.1
  (13 shorter events, 0.2 us)
Async XLA Ops:
  7.2 76.4 %all-gather.2.cloned.1.call-start = ((), (), s32[]{:S(2)}) async-start(), calls=%async_computation.2 | async-start | bytes 8912896 | tf_op jit(solution)/shard_map/all_gather | solution.py:11
  102.6 13.6 %copy-start = (s32[2]{0:T(128)S(1)}, s32[2]{0:T(128)}, u32[]{:S(2)}) copy-start(s32[2]{0:T(128)} %param.11) | copy-start | bytes 28
  102.6 20.7 %copy-start.2 = (s32[2,1]{0,1:T(1,128)S(1)}, s32[2,1]{0,1:T(1,128)}, u32[]{:S(2)}) copy-start(s32[2,1]{0,1:T(1,128)} %param.12) | copy-start | bytes 28
  102.6 33.7 %copy-start.1 = (f32[4]{0:T(128)S(1)}, f32[4]{0:T(128)}, u32[]{:S(2)}) copy-start(f32[4]{0:T(128)} %param.13) | copy-start | bytes 52
  111.9 10.4 %all-to-all-start = ((f32[8,4,1024]{2,1,0:T(4,128)}), f32[8,4,1024]{2,1,0:T(4,128)S(1)}, u32[]{:S(2)}, u32[]{:S(2)}) async-start(f32[8,4,1024]{2,1,0:T(4,128)} %broadcast_in_dim.13), calls=%async_computation | async-start | bytes 262144 | tf_op jit(solution)/shard_map/all_to_all | solution.py:39
Sparse Core Ops, SparseCore 0:
  10.1 73.4 all-gather.1

commit v4 on v2

--- a/solution.py
+++ b/solution.py
@@ -4,45 +4,92 @@
 from jax.sharding import PartitionSpec as P
 
 
+RING = 4
+SLOTS = (0, 3, 1, 2)
+
+
+def ring_step(pieces, along, step):
+    def target(index):
+        z, y = divmod(index, RING)
+        if along == "z":
+            return ((z + step) % RING) * RING + y
+        return z * RING + (y + step) % RING
+
+    return lax.ppermute(pieces, "dp", [(i, target(i)) for i in range(RING * RING)])
+
+
+def ring_gather(block, along):
+    from_before = ring_step(block, along, 1)
+    from_after = ring_step(block, along, RING - 1)
+    half = block.shape[0] // 2
+    far = jnp.concatenate(
+        [ring_step(from_before[:half], along, 1), ring_step(from_after[half:], along, RING - 1)], axis=0
+    )
+    return jnp.concatenate([block, from_before, from_after, far], axis=0)
+
+
+def combine(stats):
+    tops = stats[:, 0]
+    top = jnp.max(tops, axis=0)
+    factor = jnp.exp(tops - top[None, :])
+    total = jnp.sum(stats[:, 1] * factor, axis=0)
+    spread = jnp.sum(factor * (stats[:, 2] + stats[:, 1] * (tops - top[None, :])), axis=0)
+    chosen = jnp.sum(stats[:, 3], axis=0)
+    return jnp.stack([top, total, spread, chosen], axis=0)
+
+
 def per_device(hidden, norm_gain, head, targets, lengths, groups, baseline):
     seq_count, slot_count, width = hidden.shape
     total_rows = seq_count * slot_count
     block = min(512, total_rows)
-    weights = lax.all_gather(head, "dp", axis=0, tiled=True)
-    vocab_width = weights.shape[1]
+    vocab_width = head.shape[1]
+    split = vocab_width // 2
+    weights_a = ring_gather(ring_gather(head[:, :split], "z"), "y")
+    weights_b = ring_gather(ring_gather(head[:, split:], "y"), "z")
     offset = lax.axis_index("vocab") * vocab_width
+    here = lax.axis_index("dp")
+    here_z, here_y = here // RING, here % RING
     flat = hidden.reshape(total_rows, width).astype(jnp.float32)
     square = jnp.mean(flat * flat, axis=-1, keepdims=True)
     normed = (flat * lax.rsqrt(square + 1e-05) * norm_gain[None, :]).astype(jnp.bfloat16)
+    grid = normed.reshape(total_rows, RING, RING, width // (RING * RING))
+    grid = jnp.roll(grid, (-here_z, -here_y), axis=(1, 2))
+    order = jnp.array(SLOTS, dtype=jnp.int32)
+    grid = jnp.take(jnp.take(grid, order, axis=1), order, axis=2)
+    normed_b = grid.reshape(total_rows, width)
+    normed_a = jnp.transpose(grid, (0, 2, 1, 3)).reshape(total_rows, width)
     positions = jnp.arange(slot_count, dtype=jnp.int32)
     live = (positions[None, :] < lengths[:, None]).reshape(total_rows)
     wanted = targets.reshape(total_rows)
     column = jnp.arange(vocab_width, dtype=jnp.int32) + offset
 
-    def local_stats(rows, picks):
+    def half_stats(rows, weights, picks, columns):
         logits = jnp.dot(rows, weights, preferred_element_type=jnp.float32)
         local_top = jnp.max(logits, axis=-1)
         shifted = logits - local_top[:, None]
         expo = jnp.exp(shifted)
         local_total = jnp.sum(expo, axis=-1)
         local_spread = jnp.sum(expo * shifted, axis=-1)
-        chosen = jnp.sum(jnp.where(column[None, :] == picks[:, None], logits, 0.0), axis=-1)
+        chosen = jnp.sum(jnp.where(columns[None, :] == picks[:, None], logits, 0.0), axis=-1)
         return jnp.stack([local_top, local_total, local_spread, chosen], axis=0)
 
-    parts = [
-        local_stats(normed[start : start + block], wanted[start : start + block])
-        for start in range(0, total_rows, block)
-    ]
+    def local_stats(start):
+        picks = wanted[start : start + block]
+        both = jnp.stack(
+            [
+                half_stats(normed_a[start : start + block], weights_a, picks, column[:split]),
+                half_stats(normed_b[start : start + block], weights_b, picks, column[split:]),
+            ],
+            axis=0,
+        )
+        return combine(both)
+
+    parts = [local_stats(start) for start in range(0, total_rows, block)]
     stats = jnp.concatenate(parts, axis=1)
     vocab_count = lax.axis_size("vocab")
     spread_out = jnp.broadcast_to(stats[None], (vocab_count,) + stats.shape)
     gathered = lax.all_to_all(spread_out, "vocab", 0, 0, tiled=False)
-    tops = gathered[:, 0]
-    top = jnp.max(tops, axis=0)
-    factor = jnp.exp(tops - top[None, :])
-    total = jnp.sum(gathered[:, 1] * factor, axis=0)
-    spread = jnp.sum(factor * (gathered[:, 2] + gathered[:, 1] * (tops - top[None, :])), axis=0)
-    target = jnp.sum(gathered[:, 3], axis=0)
+    top, total, spread, target = combine(gathered)
     log_total = jnp.log(total)
     logprob = target - top - log_total
     entropy = log_total - spread / total

time: 137 us -> 184 us (1.34)
  local copies, waits for them, and re-layouts: 1.47 us -> 61.2 us
  waiting for transfers between devices: 77.4 us -> 46.9 us
  starting transfers between devices: 4.3 us -> 29.9 us
  between operations: 14.2 us -> 1.04 us
  matrix products: 14.5 us -> 18 us
  other arithmetic: 12.4 us -> 14.5 us
    all_gather x1 -> x0, waiting for transfers between devices: 70.6 us -> none  [per_device(): weights = lax.all_gather(head, 'dp', axis=0, tiled=True)]
    ppermute x0 -> x16, waiting for transfers between devices: none -> 40.8 us  [ring_step(): lax.ppermute(pieces, 'dp', [(i, target(i)) for i in range(RING * RING)])]
    ppermute x0 -> x16, starting transfers between devices: none -> 25.6 us  [ring_step(): lax.ppermute(pieces, 'dp', [(i, target(i)) for i in range(RING * RING)])]
    concatenate x0 -> x4, local copies, waits for them, and re-layouts: none -> 25.1 us  [ring_gather(): return jnp.concatenate([block, from_before, from_after, far], axis=0)]
    slice x1 -> x13, local copies, waits for them, and re-layouts: 0.77 us -> 14.4 us  [the longest x4 5.96 us: ring_gather(): from_after[half:]]
    convert_element_type x0 -> x2, local copies, waits for them, and re-layouts: none -> 10.9 us  [per_device(): flat = hidden.reshape(total_rows, width).astype(jnp.float32)]
    gather x0 -> x3, local copies, waits for them, and re-layouts: none -> 7.53 us  [per_device(): grid = jnp.take(jnp.take(grid, order, axis=1), order, axis=2)]
    dot_general x2 -> x4, matrix products: 14.4 us -> 17.8 us  [half_stats(): logits = jnp.dot(rows, weights, preferred_element_type=jnp.float32)]
  transfers between devices with their start and end apart: 2 -> 17, of which waited for: 2 -> 6; matrix products, arithmetic and copies ran while one was open for 4% -> 36% of each run, Pallas kernels for 0% -> 0%
where the time goes in v4:
time: 184 us; the launch traced here: 183 us
  local copies, waits for them, and re-layouts  61.2 us (33%)
  waiting for transfers between devices  46.9 us (25%)
  starting transfers between devices  29.9 us (16%)
  matrix products  18 us (10%)
  other arithmetic  14.5 us (8%)
  blocking collectives  11.4 us (6%)
    ppermute x16, waiting for transfers between devices, ring_step(): lax.ppermute(pieces, 'dp', [(i, target(i)) for i in range(RING * RING)])  40.8 us
    ppermute x16, starting transfers between devices, ring_step(): lax.ppermute(pieces, 'dp', [(i, target(i)) for i in range(RING * RING)])  25.6 us
    concatenate x4, local copies, waits for them, and re-layouts, ring_gather(): return jnp.concatenate([block, from_before, from_after, far], axis=0)  25.1 us
    dot_general x4, matrix products, half_stats(): logits = jnp.dot(rows, weights, preferred_element_type=jnp.float32)  17.8 us
    all_to_all x1, blocking collectives, per_device(): lax.all_to_all(partial_out, 'dp', 0, 0, tiled=False)  11.4 us
    convert_element_type x2, local copies, waits for them, and re-layouts, per_device(): flat = hidden.reshape(total_rows, width).astype(jnp.float32)  10.9 us
    gather x3, local copies, waits for them, and re-layouts, per_device(): grid = jnp.take(jnp.take(grid, order, axis=1), order, axis=2)  7.53 us
    reduce_sum x1, other arithmetic, half_stats(): local_total = jnp.sum(expo, axis=-1)  6.51 us
  transfers between devices with their start and end apart: 17, of which 6 were waited for; matrix products, arithmetic and copies ran while one was open for 36% of the time, Pallas kernels for 0%

profile of v4, /device:TPU:0, one launch (start us, length us, event | category | flops | bytes accessed | tf_op | source)
XLA Modules:
  0.0 183.0 jit_solution(9573939482930329380)
XLA Ops:
  3.0 4.1 %collective-permute-start.1 = (bf16[64,2000]{0,1:T(8,128)(2,1)}, bf16[64,2000]{0,1:T(8,128)(2,1)}, u32[]{:S(2)}, u32[]{:S(2)}) collective-permute-start(bf16[64,2000]{0,1:T(8,128)(2,1)} %copy.71), channel_id=1, source_target_pairs={{0,96},{8,104},{16,112},{24,120},{32,0},{40,8},{48,16},{56,24},{64... | collective-permute-start | bytes 768008 | tf_op jit(solution)/shard_map/ppermute | solution.py:18
  7.5 3.1 %collective-permute-start.9 = (bf16[64,2000]{0,1:T(8,128)(2,1)S(1)}, bf16[64,2000]{0,1:T(8,128)(2,1)S(1)}, u32[]{:S(2)}, u32[]{:S(2)}) collective-permute-start(bf16[64,2000]{0,1:T(8,128)(2,1)S(1)} %copy.72), channel_id=1, source_target_pairs={{0,24},{8,0},{16,8},{24,16},{32,56},{40,32},{48,40},{56,48},{64,88... | collective-permute-start | bytes 768008 | tf_op jit(solution)/shard_map/ppermute | solution.py:18
  12.6 4.3 %copy.58 = f32[2,512,1024]{1,0,2:T(2,128)} copy(bf16[2,512,1024]{2,1,0:T(8,128)(2,1)S(1)} %copy-done) | data formatting | bytes 6291456 | tf_op jit(solution)/shard_map/convert_element_type | solution.py:52
  17.0 6.6 %reshape.103 = f32[1024,4,4,64]{0,3,2,1:T(8,128)} reshape(f32[2,512,1024]{1,0,2:T(2,128)} %copy.58) | data formatting | bytes 8388608 | tf_op jit(solution)/shard_map/convert_element_type | solution.py:52
  25.7 3.2 %collective-permute-start.3 = (bf16[32,2000]{0,1:T(8,128)(2,1)}, bf16[32,2000]{0,1:T(8,128)(2,1)}, u32[]{:S(2)}, u32[]{:S(2)}) collective-permute-start(bf16[32,2000]{0,1:T(8,128)(2,1)} %slice.160), channel_id=1, source_target_pairs={{0,96},{8,104},{16,112},{24,120},{32,0},{40,8},{48,16},{56,24},{64... | collective-permute-start | bytes 384008 | tf_op jit(solution)/shard_map/ppermute | solution.py:18
  31.7 7.7 %collective-permute-done.3 = bf16[32,2000]{0,1:T(8,128)(2,1)} collective-permute-done((bf16[32,2000]{0,1:T(8,128)(2,1)}, bf16[32,2000]{0,1:T(8,128)(2,1)}, u32[]{:S(2)}, u32[]{:S(2)}) %collective-permute-start.3) | collective-permute-done | bytes 128032 | tf_op jit(solution)/shard_map/ppermute | solution.py:18
  39.4 3.4 %collective-permute-done.2 = bf16[32,2000]{0,1:T(8,128)(2,1)} collective-permute-done((bf16[32,2000]{0,1:T(8,128)(2,1)}, bf16[32,2000]{0,1:T(8,128)(2,1)}, u32[]{:S(2)}, u32[]{:S(2)}) %collective-permute-start.2) | collective-permute-done | bytes 128032 | tf_op jit(solution)/shard_map/ppermute | solution.py:18
  42.8 4.2 %concatenate.28 = bf16[256,2000]{0,1:T(8,128)(2,1)} concatenate(bf16[64,2000]{0,1:T(8,128)(2,1)} %copy.71, bf16[64,2000]{0,1:T(8,128)(2,1)} %collective-permute-done, bf16[64,2000]{0,1:T(8,128)(2,1)} %collective-permute-done.1, bf16[32,2000]{0,1:T(8,128)(2,1)} %collective-permute-done.2, bf16[32,2000]{0,1:T(8,128)(2,1)} %collective-permute-done.3), dimensions={0} | concatenate | bytes 2048000 | tf_op jit(solution)/shard_map/concatenate | solution.py:28
  47.2 2.9 %collective-permute-start.5 = (bf16[256,2000]{0,1:T(8,128)(2,1)}, bf16[256,2000]{0,1:T(8,128)(2,1)}, u32[]{:S(2)}, u32[]{:S(2)}) collective-permute-start(bf16[256,2000]{0,1:T(8,128)(2,1)} %concatenate.28), channel_id=1, source_target_pairs={{0,24},{8,0},{16,8},{24,16},{32,56},{40,32},{48,40},{56,48},{64,88... | collective-permute-start | bytes 3072008 | tf_op jit(solution)/shard_map/ppermute | solution.py:18
  56.7 3.2 %copy.59 = bf16[1024,4,4,64]{0,3,1,2:T(8,128)(2,1)} copy(bf16[1024,4,4,64]{0,3,2,1:T(8,128)(2,1)} %bitcast.129) | data formatting | bytes 4194304 | tf_op jit(solution)/shard_map/jit(_take)/gather | solution.py:58
  62.3 18.8 %collective-permute-done.11 = bf16[32,2000]{0,1:T(8,128)(2,1)} collective-permute-done((bf16[32,2000]{0,1:T(8,128)(2,1)}, bf16[32,2000]{0,1:T(8,128)(2,1)}, u32[]{:S(2)}, u32[]{:S(2)}) %collective-permute-start.11) | collective-permute-done | bytes 128032 | tf_op jit(solution)/shard_map/ppermute | solution.py:18
  81.8 4.5 %concatenate.30 = bf16[256,2000]{0,1:T(8,128)(2,1)} concatenate(bf16[64,2000]{0,1:T(8,128)(2,1)S(1)} %copy.72, bf16[64,2000]{0,1:T(8,128)(2,1)} %collective-permute-done.8, bf16[64,2000]{0,1:T(8,128)(2,1)S(1)} %collective-permute-done.9, bf16[32,2000]{0,1:T(8,128)(2,1)} %collective-permute-done.10, bf16[32,2000]{0,1:T(8,128)(2,1)} %collective-permute-done.11), dimensions={0} | concatenate | bytes 2048000 | tf_op jit(solution)/shard_map/concatenate | solution.py:28
  86.4 3.2 %collective-permute-start.13 = (bf16[256,2000]{0,1:T(8,128)(2,1)}, bf16[256,2000]{0,1:T(8,128)(2,1)}, u32[]{:S(2)}, u32[]{:S(2)}) collective-permute-start(bf16[256,2000]{0,1:T(8,128)(2,1)} %concatenate.30), channel_id=1, source_target_pairs={{0,96},{8,104},{16,112},{24,120},{32,0},{40,8},{48,16},{56,24},{64... | collective-permute-start | bytes 3072008 | tf_op jit(solution)/shard_map/ppermute | solution.py:18
  99.3 10.1 %collective-permute-done.12 = bf16[256,2000]{0,1:T(8,128)(2,1)} collective-permute-done((bf16[256,2000]{0,1:T(8,128)(2,1)}, bf16[256,2000]{0,1:T(8,128)(2,1)}, u32[]{:S(2)}, u32[]{:S(2)}) %collective-permute-start.12) | collective-permute-done | bytes 1024032 | tf_op jit(solution)/shard_map/ppermute | solution.py:18
  113.2 3.2 %collective-permute-start.15 = (bf16[128,2000]{0,1:T(8,128)(2,1)}, bf16[128,2000]{0,1:T(8,128)(2,1)S(1)}, u32[]{:S(2)}, u32[]{:S(2)}) collective-permute-start(bf16[128,2000]{0,1:T(8,128)(2,1)} %slice.168), channel_id=1, source_target_pairs={{0,96},{8,104},{16,112},{24,120},{32,0},{40,8},{48,16},{56,24},{64... | collective-permute-start | bytes 1536008 | tf_op jit(solution)/shard_map/ppermute | solution.py:18
  116.4 8.3 %concatenate.29 = bf16[1024,2000]{0,1:T(8,128)(2,1)} concatenate(bf16[64,2000]{0,1:T(8,128)(2,1)} %copy.71, bf16[64,2000]{0,1:T(8,128)(2,1)} %collective-permute-done, bf16[64,2000]{0,1:T(8,128)(2,1)} %collective-permute-done.1, bf16[32,2000]{0,1:T(8,128)(2,1)} %collective-permute-done.2, bf16[32,2000]{0,1:T(8,128)(2,1)} %collective-permute-done.3, ...), dimensions={0} | concatenate | bytes 8192000 | tf_op jit(solution)/shard_map/concatenate | solution.py:28
  124.7 6.5 %fusion.56 = (f32[512]{0:T(512)S(1)}, f32[512,2000]{0,1:T(8,128)}) fusion(bf16[1024,2000]{0,1:T(8,128)(2,1)} %concatenate.29, bf16[512,1024]{0,1:T(8,128)(2,1)S(1)} %bitcast.133), kind=kOutput, calls=%fused_computation.116 | convolution fusion | flops 2098175488 | bytes 9242624 | tf_op jit(solution)/shard_map/dot_general | solution.py:67
  131.2 4.3 %fusion.55 = (f32[512]{0:T(512)S(1)}, f32[512,2000]{0,1:T(8,128)}) fusion(bf16[1024,2000]{0,1:T(8,128)(2,1)S(1)} %copy-done.1, bf16[512,1024]{0,1:T(8,128)(2,1)S(1)} %bitcast.132), kind=kOutput, calls=%fused_computation.115 | convolution fusion | flops 2098175488 | bytes 9242624 | tf_op jit(solution)/shard_map/dot_general | solution.py:67
  135.5 8.2 %concatenate.31 = bf16[1024,2000]{0,1:T(8,128)(2,1)} concatenate(bf16[64,2000]{0,1:T(8,128)(2,1)S(1)} %copy.72, bf16[64,2000]{0,1:T(8,128)(2,1)} %collective-permute-done.8, bf16[64,2000]{0,1:T(8,128)(2,1)S(1)} %collective-permute-done.9, bf16[32,2000]{0,1:T(8,128)(2,1)} %collective-permute-done.10, bf16[32,2000]{0,1:T(8,128)(2,1)} %collective-permute-done.11, ...), dimensions={0} | concatenate | bytes 8192000 | tf_op jit(solution)/shard_map/concatenate | solution.py:28
  143.7 4.7 %fusion.54 = (f32[512]{0:T(512)S(1)}, f32[512,2000]{0,1:T(8,128)S(1)}) fusion(bf16[1024,2000]{0,1:T(8,128)(2,1)} %concatenate.31, bf16[512,1024]{0,1:T(8,128)(2,1)S(1)} %bitcast.131), kind=kOutput, calls=%fused_computation.114 | convolution fusion | flops 2098175488 | bytes 9242624 | tf_op jit(solution)/shard_map/dot_general | solution.py:67
  151.9 6.5 %exponential_reduce_fusion.2 = (f32[512]{0:T(512)S(1)}, f32[512]{0:T(512)S(1)}, f32[512]{0:T(512)S(1)}, f32[512]{0:T(512)S(1)}, f32[512]{0:T(512)S(1)}, /*index=...) fusion(f32[512,2000]{0,1:T(8,128)S(1)} %get-tuple-element.65, ...), kind=kLoop, calls=%fused_computation.7 | loop fusion | flops 28665856 | bytes 16436864 | tf_op jit(solution)/shard_map/reduce_sum | solution.py:71
  159.3 4.3 %all-to-all-start = ((f32[8,4,1024]{2,1,0:T(4,128)}), f32[8,4,1024]{2,1,0:T(4,128)S(1)}, u32[]{:S(2)}, u32[]{:S(2)}) async-start(f32[8,4,1024]{2,1,0:T(4,128)} %broadcast_in_dim.40), calls=%async_computation | async-start | bytes 262144 | tf_op jit(solution)/shard_map/all_to_all | solution.py:91
  163.6 6.1 %all-to-all-done = f32[8,4,1024]{2,1,0:T(4,128)S(1)} async-done(((f32[8,4,1024]{2,1,0:T(4,128)}), f32[8,4,1024]{2,1,0:T(4,128)S(1)}, u32[]{:S(2)}, u32[]{:S(2)}) %all-to-all-start) | async-done | bytes 131104 | tf_op jit(solution)/shard_map/all_to_all | solution.py:91
  171.0 11.4 %all_to_all.10 = f32[16,4,3]{1,2,0:T(4,128)S(1)} all-to-all(f32[16,4,3]{1,2,0:T(4,128)S(1)} %broadcast_in_dim.42), channel_id=1, replica_groups=mesh['dp'=16,'vocab'=8] {'dp'}, dimensions={0} | all-to-all | bytes 1536 | tf_op jit(solution)/shard_map/all_to_all | solution.py:108
  (105 shorter events, 38.9 us)
Async XLA Ops:
  0.6 12.0 %copy-start = (bf16[2,512,1024]{2,1,0:T(8,128)(2,1)S(1)}, bf16[2,512,1024]{2,1,0:T(8,128)(2,1)}, u32[]{:S(2)}) copy-start(bf16[2,512,1024]{2,1,0:T(8,128)(2,1)} %param.8) | copy-start | bytes 6291460
  3.0 20.7 %collective-permute-start.1 = (bf16[64,2000]{0,1:T(8,128)(2,1)}, bf16[64,2000]{0,1:T(8,128)(2,1)}, u32[]{:S(2)}, u32[]{:S(2)}) collective-permute-start(bf16[64,2000]{0,1:T(8,128)(2,1)} %copy.71), channel_id=1, source_target_pairs={{0,96},{8,104},{16,112},{24,120},{32,0},{40,8},{48,16},{56,24},{64... | collective-permute-start | bytes 768008 | tf_op jit(solution)/shard_map/ppermute | solution.py:18
  7.2 21.8 %collective-permute-start = (bf16[64,2000]{0,1:T(8,128)(2,1)}, bf16[64,2000]{0,1:T(8,128)(2,1)}, u32[]{:S(2)}, u32[]{:S(2)}) collective-permute-start(bf16[64,2000]{0,1:T(8,128)(2,1)} %copy.71), channel_id=1, source_target_pairs={{0,32},{8,40},{16,48},{24,56},{32,64},{40,72},{48,80},{56,88},{64,... | collective-permute-start | bytes 768008 | tf_op jit(solution)/shard_map/ppermute | solution.py:18
  7.5 43.5 %collective-permute-start.9 = (bf16[64,2000]{0,1:T(8,128)(2,1)S(1)}, bf16[64,2000]{0,1:T(8,128)(2,1)S(1)}, u32[]{:S(2)}, u32[]{:S(2)}) collective-permute-start(bf16[64,2000]{0,1:T(8,128)(2,1)S(1)} %copy.72), channel_id=1, source_target_pairs={{0,24},{8,0},{16,8},{24,16},{32,56},{40,32},{48,40},{56,48},{64,88... | collective-permute-start | bytes 768008 | tf_op jit(solution)/shard_map/ppermute | solution.py:18
  10.5 43.1 %collective-permute-start.8 = (bf16[64,2000]{0,1:T(8,128)(2,1)S(1)}, bf16[64,2000]{0,1:T(8,128)(2,1)}, u32[]{:S(2)}, u32[]{:S(2)}) collective-permute-start(bf16[64,2000]{0,1:T(8,128)(2,1)S(1)} %copy.72), channel_id=1, source_target_pairs={{0,8},{8,16},{16,24},{24,0},{32,40},{40,48},{48,56},{56,32},{64,72... | collective-permute-start | bytes 768008 | tf_op jit(solution)/shard_map/ppermute | solution.py:18
  25.7 13.6 %collective-permute-start.3 = (bf16[32,2000]{0,1:T(8,128)(2,1)}, bf16[32,2000]{0,1:T(8,128)(2,1)}, u32[]{:S(2)}, u32[]{:S(2)}) collective-permute-start(bf16[32,2000]{0,1:T(8,128)(2,1)} %slice.160), channel_id=1, source_target_pairs={{0,96},{8,104},{16,112},{24,120},{32,0},{40,8},{48,16},{56,24},{64... | collective-permute-start | bytes 384008 | tf_op jit(solution)/shard_map/ppermute | solution.py:18
  29.0 13.8 %collective-permute-start.2 = (bf16[32,2000]{0,1:T(8,128)(2,1)}, bf16[32,2000]{0,1:T(8,128)(2,1)}, u32[]{:S(2)}, u32[]{:S(2)}) collective-permute-start(bf16[32,2000]{0,1:T(8,128)(2,1)} %bitcast.126), channel_id=1, source_target_pairs={{0,32},{8,40},{16,48},{24,56},{32,64},{40,72},{48,80},{56,88},{64,... | collective-permute-start | bytes 384008 | tf_op jit(solution)/shard_map/ppermute | solution.py:18
  46.9 45.2 %collective-permute-start.4 = (bf16[256,2000]{0,1:T(8,128)(2,1)}, bf16[256,2000]{0,1:T(8,128)(2,1)}, u32[]{:S(2)}, u32[]{:S(2)}) collective-permute-start(bf16[256,2000]{0,1:T(8,128)(2,1)} %concatenate.28), channel_id=1, source_target_pairs={{0,8},{8,16},{16,24},{24,0},{32,40},{40,48},{48,56},{56,32},{64,72... | collective-permute-start | bytes 3072008 | tf_op jit(solution)/shard_map/ppermute | solution.py:18
  47.2 46.9 %collective-permute-start.5 = (bf16[256,2000]{0,1:T(8,128)(2,1)}, bf16[256,2000]{0,1:T(8,128)(2,1)}, u32[]{:S(2)}, u32[]{:S(2)}) collective-permute-start(bf16[256,2000]{0,1:T(8,128)(2,1)} %concatenate.28), channel_id=1, source_target_pairs={{0,24},{8,0},{16,8},{24,16},{32,56},{40,32},{48,40},{56,48},{64,88... | collective-permute-start | bytes 3072008 | tf_op jit(solution)/shard_map/ppermute | solution.py:18
  51.9 29.2 %collective-permute-start.11 = (bf16[32,2000]{0,1:T(8,128)(2,1)}, bf16[32,2000]{0,1:T(8,128)(2,1)}, u32[]{:S(2)}, u32[]{:S(2)}) collective-permute-start(bf16[32,2000]{0,1:T(8,128)(2,1)} %slice.166), channel_id=1, source_target_pairs={{0,24},{8,0},{16,8},{24,16},{32,56},{40,32},{48,40},{56,48},{64,88... | collective-permute-start | bytes 384008 | tf_op jit(solution)/shard_map/ppermute | solution.py:18
  53.7 28.2 %collective-permute-start.10 = (bf16[32,2000]{0,1:T(8,128)(2,1)}, bf16[32,2000]{0,1:T(8,128)(2,1)}, u32[]{:S(2)}, u32[]{:S(2)}) collective-permute-start(bf16[32,2000]{0,1:T(8,128)(2,1)} %bitcast.125), channel_id=1, source_target_pairs={{0,8},{8,16},{16,24},{24,0},{32,40},{40,48},{48,56},{56,32},{64,72... | collective-permute-start | bytes 384008 | tf_op jit(solution)/shard_map/ppermute | solution.py:18
  86.4 23.1 %collective-permute-start.12 = (bf16[256,2000]{0,1:T(8,128)(2,1)}, bf16[256,2000]{0,1:T(8,128)(2,1)}, u32[]{:S(2)}, u32[]{:S(2)}) collective-permute-start(bf16[256,2000]{0,1:T(8,128)(2,1)} %concatenate.30), channel_id=1, source_target_pairs={{0,32},{8,40},{16,48},{24,56},{32,64},{40,72},{48,80},{56,88},{64,... | collective-permute-start | bytes 3072008 | tf_op jit(solution)/shard_map/ppermute | solution.py:18
  86.4 25.0 %collective-permute-start.13 = (bf16[256,2000]{0,1:T(8,128)(2,1)}, bf16[256,2000]{0,1:T(8,128)(2,1)}, u32[]{:S(2)}, u32[]{:S(2)}) collective-permute-start(bf16[256,2000]{0,1:T(8,128)(2,1)} %concatenate.30), channel_id=1, source_target_pairs={{0,96},{8,104},{16,112},{24,120},{32,0},{40,8},{48,16},{56,24},{64... | collective-permute-start | bytes 3072008 | tf_op jit(solution)/shard_map/ppermute | solution.py:18
  89.9 7.8 %copy-start.10 = (s32[2,512]{1,0:T(2,128)S(1)}, s32[2,512]{1,0:T(2,128)}, u32[]{:S(2)}) copy-start(s32[2,512]{1,0:T(2,128)} %param.11) | copy-start | bytes 12292
  93.2 23.2 %collective-permute-start.6 = (bf16[128,2000]{0,1:T(8,128)(2,1)S(1)}, bf16[128,2000]{0,1:T(8,128)(2,1)}, u32[]{:S(2)}, u32[]{:S(2)}) collective-permute-start(bf16[128,2000]{0,1:T(8,128)(2,1)S(1)} %slice.161), channel_id=1, source_target_pairs={{0,8},{8,16},{16,24},{24,0},{32,40},{40,48},{48,56},{56,32},{64,72... | collective-permute-start | bytes 1536008 | tf_op jit(solution)/shard_map/ppermute | solution.py:18
  95.3 21.2 %collective-permute-start.7 = (bf16[128,2000]{0,1:T(8,128)(2,1)S(1)}, bf16[128,2000]{0,1:T(8,128)(2,1)}, u32[]{:S(2)}, u32[]{:S(2)}) collective-permute-start(bf16[128,2000]{0,1:T(8,128)(2,1)S(1)} %slice.162), channel_id=1, source_target_pairs={{0,24},{8,0},{16,8},{24,16},{32,56},{40,32},{48,40},{56,48},{64,88... | collective-permute-start | bytes 1536008 | tf_op jit(solution)/shard_map/ppermute | solution.py:18
  111.3 24.2 %collective-permute-start.14 = (bf16[128,2000]{0,1:T(8,128)(2,1)}, bf16[128,2000]{0,1:T(8,128)(2,1)S(1)}, u32[]{:S(2)}, u32[]{:S(2)}) collective-permute-start(bf16[128,2000]{0,1:T(8,128)(2,1)} %slice.167), channel_id=1, source_target_pairs={{0,32},{8,40},{16,48},{24,56},{32,64},{40,72},{48,80},{56,88},{64,... | collective-permute-start | bytes 1536008 | tf_op jit(solution)/shard_map/ppermute | solution.py:18
  113.2 11.5 %copy-start.8 = (bf16[512,4,4,64]{0,3,2,1:T(8,128)(2,1)S(1)}, bf16[512,4,4,64]{0,3,2,1:T(8,128)(2,1)}, u32[]{:S(2)}) copy-start(bf16[512,4,4,64]{0,3,2,1:T(8,128)(2,1)} %get-tuple-element.31) | copy-start | bytes 3145732
  113.2 22.4 %collective-permute-start.15 = (bf16[128,2000]{0,1:T(8,128)(2,1)}, bf16[128,2000]{0,1:T(8,128)(2,1)S(1)}, u32[]{:S(2)}, u32[]{:S(2)}) collective-permute-start(bf16[128,2000]{0,1:T(8,128)(2,1)} %slice.168), channel_id=1, source_target_pairs={{0,96},{8,104},{16,112},{24,120},{32,0},{40,8},{48,16},{56,24},{64... | collective-permute-start | bytes 1536008 | tf_op jit(solution)/shard_map/ppermute | solution.py:18
  135.5 8.2 %copy-start.6 = (bf16[512,4,4,64]{0,3,2,1:T(8,128)(2,1)S(1)}, bf16[512,4,4,64]{0,3,2,1:T(8,128)(2,1)}, u32[]{:S(2)}) copy-start(bf16[512,4,4,64]{0,3,2,1:T(8,128)(2,1)} %copy.63) | copy-start | bytes 3145732
  151.9 11.8 %copy-start.11 = (s32[2]{0:T(128)S(1)}, s32[2]{0:T(128)}, u32[]{:S(2)}) copy-start(s32[2]{0:T(128)} %param.12) | copy-start | bytes 28
  151.9 18.9 %copy-start.14 = (s32[2,1]{0,1:T(1,128)S(1)}, s32[2,1]{0,1:T(1,128)}, u32[]{:S(2)}) copy-start(s32[2,1]{0,1:T(1,128)} %param.13) | copy-start | bytes 28
  151.9 30.6 %copy-start.13 = (f32[4]{0:T(128)S(1)}, f32[4]{0:T(128)}, u32[]{:S(2)}) copy-start(f32[4]{0:T(128)} %param.14) | copy-start | bytes 52
  159.3 10.4 %all-to-all-start = ((f32[8,4,1024]{2,1,0:T(4,128)}), f32[8,4,1024]{2,1,0:T(4,128)S(1)}, u32[]{:S(2)}, u32[]{:S(2)}) async-start(f32[8,4,1024]{2,1,0:T(4,128)} %broadcast_in_dim.40), calls=%async_computation | async-start | bytes 262144 | tf_op jit(solution)/shard_map/all_to_all | solution.py:91
  (8 other events, 42.7 us)

commit v5 on v3

--- a/solution.py
+++ b/solution.py
@@ -1,15 +1,67 @@
+import functools
+
 import jax
 import jax.numpy as jnp
 from jax import lax
+from jax.experimental import pallas as pl
+from jax.experimental.pallas import tpu as pltpu
 from jax.sharding import PartitionSpec as P
+
+LANE = 128
+CHUNK = 512
+
+
+def stats_kernel(x_ref, w_ref, p_ref, o_ref, *, valid):
+    x = x_ref[...]
+    picks = p_ref[...]
+    rows, width = x.shape[0], w_ref.shape[1]
+    top = total = spread = chosen = None
+    for k in range(width // CHUNK):
+        logits = jnp.dot(x, w_ref[:, k * CHUNK : (k + 1) * CHUNK], preferred_element_type=jnp.float32)
+        cols = lax.broadcasted_iota(jnp.int32, (rows, CHUNK), 1) + k * CHUNK
+        hit = jnp.sum(jnp.where(cols == picks, logits, 0.0), axis=1, keepdims=True)
+        if (k + 1) * CHUNK > valid:
+            logits = jnp.where(cols < valid, logits, -1e30)
+        chunk_top = jnp.max(logits, axis=1, keepdims=True)
+        if top is None:
+            shifted = logits - chunk_top
+            expo = jnp.exp(shifted)
+            top, chosen = chunk_top, hit
+            total = jnp.sum(expo, axis=1, keepdims=True)
+            spread = jnp.sum(expo * shifted, axis=1, keepdims=True)
+        else:
+            new_top = jnp.maximum(top, chunk_top)
+            factor = jnp.exp(top - new_top)
+            shifted = logits - new_top
+            expo = jnp.exp(shifted)
+            spread = factor * (spread + total * (top - new_top)) + jnp.sum(expo * shifted, axis=1, keepdims=True)
+            total = factor * total + jnp.sum(expo, axis=1, keepdims=True)
+            top, chosen = new_top, chosen + hit
+    o_ref[...] = jnp.concatenate([top, total, spread, chosen], axis=1)
+
+
+def row_stats(rows, weights, picks, valid):
+    count, width = rows.shape
+    return pl.pallas_call(
+        functools.partial(stats_kernel, valid=valid),
+        grid=(1,),
+        in_specs=[
+            pl.BlockSpec((count, width), lambda i: (0, 0)),
+            pl.BlockSpec(weights.shape, lambda i: (0, 0)),
+            pl.BlockSpec((count, 1), lambda i: (0, 0)),
+        ],
+        out_specs=pl.BlockSpec((count, 4), lambda i: (0, 0)),
+        out_shape=jax.ShapeDtypeStruct((count, 4), jnp.float32),
+        compiler_params=pltpu.CompilerParams(vmem_limit_bytes=48 * 1024 * 1024),
+    )(rows, weights, picks.reshape(count, 1))
 
 
 def per_device(hidden, norm_gain, head, targets, lengths, groups, baseline):
     seq_count, slot_count, width = hidden.shape
     total_rows = seq_count * slot_count
-    block = total_rows
-    weights = lax.all_gather(head, "dp", axis=0, tiled=True)
-    vocab_width = weights.shape[1]
+    vocab_width = head.shape[1]
+    padded = -(-vocab_width // CHUNK) * CHUNK
+    weights = lax.all_gather(jnp.pad(head, ((0, 0), (0, padded - vocab_width))), "dp", axis=0, tiled=True)
     offset = lax.axis_index("vocab") * vocab_width
     flat = hidden.reshape(total_rows, width).astype(jnp.float32)
     square = jnp.mean(flat * flat, axis=-1, keepdims=True)
@@ -17,23 +69,7 @@
     positions = jnp.arange(slot_count, dtype=jnp.int32)
     live = (positions[None, :] < lengths[:, None]).reshape(total_rows)
     wanted = targets.reshape(total_rows)
-    column = jnp.arange(vocab_width, dtype=jnp.int32) + offset
-
-    def local_stats(rows, picks):
-        logits = jnp.dot(rows, weights, preferred_element_type=jnp.float32)
-        local_top = jnp.max(logits, axis=-1)
-        shifted = logits - local_top[:, None]
-        expo = jnp.exp(shifted)
-        local_total = jnp.sum(expo, axis=-1)
-        local_spread = jnp.sum(expo * shifted, axis=-1)
-        chosen = jnp.sum(jnp.where(column[None, :] == picks[:, None], logits, 0.0), axis=-1)
-        return jnp.stack([local_top, local_total, local_spread, chosen], axis=0)
-
-    parts = [
-        local_stats(normed[start : start + block], wanted[start : start + block])
-        for start in range(0, total_rows, block)
-    ]
-    stats = jnp.concatenate(parts, axis=1)
+    stats = row_stats(normed, weights, wanted - offset, vocab_width).T
     vocab_count = lax.axis_size("vocab")
     spread_out = jnp.broadcast_to(stats[None], (vocab_count,) + stats.shape)
     gathered = lax.all_to_all(spread_out, "vocab", 0, 0, tiled=False)

time: 144 us -> 131 us (0.910)
  matrix products: 19.2 us -> 0.19 us
  Pallas kernels: 0 us -> 14.2 us
  other arithmetic: 14.5 us -> 6.52 us
  waiting for transfers between devices: 77.5 us -> 75.3 us
  local copies, waits for them, and re-layouts: 1.39 us -> 3.06 us
    dot_general x1 -> x0, matrix products: 19 us -> none  [local_stats(): logits = jnp.dot(rows, weights, preferred_element_type=jnp.float32)]
    pallas_call x0 -> x1, Pallas kernels: none -> 14.2 us  [row_stats(): pl.pallas_call(functools.partial(stats_kernel, valid=valid), grid=(1,), i...]
    reduce_sum x1 -> x0, other arithmetic: 8.65 us -> none  [local_stats(): local_total = jnp.sum(expo, axis=-1)]
    pad x0 -> x1, local copies, waits for them, and re-layouts: none -> 1.93 us  [per_device(): jnp.pad(head, ((0, 0), (0, padded - vocab_width)))]
    all_gather x1, waiting for transfers between devices: 70.7 us -> 69.2 us  [per_device(): lax.all_gather(jnp.pad(head, ((0, 0), (0, padded - vocab_width))), 'dp',...]
  transfers between devices with their start and end apart: 2 -> 2, of which waited for: 2 -> 2; matrix products, arithmetic and copies ran while one was open for 3% -> 4% of each run, Pallas kernels for 0% -> 0%
where the time goes in v5:
time: 131 us; the launch traced here: 130 us
  waiting for transfers between devices  75.3 us (57%)
  Pallas kernels  14.2 us (11%)
  between operations  14.1 us (11%)
  blocking collectives  12.7 us (10%)
  other arithmetic  6.52 us (5%)
  starting transfers between devices  4.29 us (3%)
  local copies, waits for them, and re-layouts  3.06 us (2%)
    all_gather x1, waiting for transfers between devices, per_device(): lax.all_gather(jnp.pad(head, ((0, 0), (0, padded - vocab_width))), 'dp',...  69.2 us
    pallas_call x1, Pallas kernels, row_stats(): pl.pallas_call(functools.partial(stats_kernel, valid=valid), grid=(1,), i...  14.2 us
    all_to_all x1, blocking collectives, per_device(): lax.all_to_all(partial_out, 'dp', 0, 0, tiled=False)  12.7 us
    all_to_all x1, waiting for transfers between devices, per_device(): gathered = lax.all_to_all(spread_out, 'vocab', 0, 0, tiled=False)  6.09 us
    all_to_all x1, starting transfers between devices, per_device(): gathered = lax.all_to_all(spread_out, 'vocab', 0, 0, tiled=False)  4.25 us
  transfers between devices with their start and end apart: 2, of which 2 were waited for; matrix products, arithmetic and copies ran while one was open for 4% of the time, Pallas kernels for 0%

profile of v5, /device:TPU:0, one launch (start us, length us, event | category | flops | bytes accessed | tf_op | source)
XLA Modules:
  0.0 130.4 jit_solution(7174225601226977981)
XLA Ops:
  7.2 0.0 copy-start
  7.2 0.0 all-gather.2.cloned.1.call-start
  7.2 1.9 %pad.4 = bf16[64,4096]{1,0:T(8,128)(2,1)} pad(bf16[64,4000]{1,0:T(8,128)(2,1)} %param.9, bf16[]{:T(256)} %constant.5.clone.1), padding=0_0x0_96 | pad | bytes 1036290 | tf_op jit(solution)/shard_map/jit(_pad)/pad | solution.py:64
  9.1 0.0 all-gather.2.cloned.1.call-update
  9.2 2.1 %multiply_reduce_fusion = f32[2,512]{1,0:T(2,128)S(1)} fusion(bf16[2,512,1024]{2,1,0:T(8,128)(2,1)} %param.7), kind=kLoop, calls=%fused_computation.3 | loop fusion | flops 3144704 | bytes 2101248 | tf_op jit(solution)/shard_map/reduce_sum | solution.py:67
  11.3 0.7 subtract_bitcast_fusion
  12.0 0.2 copy.38
  12.2 0.0 copy-done
  12.2 2.1 %fusion.1.x_ref = bf16[1024,1024]{1,0:T(8,128)(2,1)S(1)} fusion(f32[1024]{0:T(1024)S(1)} %copy-done, f32[1024]{0:T(1024)S(1)} %bitcast.51, bf16[2,512,1024]{2,1,0:T(8,128)(2,1)} %param.7), kind=kLoop, calls=%fused_computation.2 | loop fusion | flops 4194304 | bytes 4202496 | tf_op jit(solution)/shard_map/convert_element_type | solution.py:68
  14.4 69.2 %all-gather.2.cloned.1.call-done.w_ref = bf16[1024,4096]{1,0:T(8,128)(2,1)} async-done(((bf16[64,4096]{1,0:T(8,128)(2,1)}), bf16[1024,4096]{1,0:T(8,128)(2,1)}) %all-gather.2.cloned.1.call-update) | async-done | bytes 8388624 | tf_op jit(solution)/shard_map/all_gather | solution.py:64
  83.6 0.0 copy-start.1
  83.6 14.2 %shard_map.94 = f32[1024,4]{1,0:T(8,128)S(1)} custom-call(bf16[1024,1024]{1,0:T(8,128)(2,1)S(1)} %fusion.1.x_ref, bf16[1024,4096]{1,0:T(8,128)(2,1)} %all-gather.2.cloned.1.call-done.w_ref, s32[1024,1]{1,0:T(8,128)S(1)} %bitcast.48), custom_call_target="tpu_custom_call" | custom-call | tf_op jit(solution)/shard_map/pallas_call | solution.py:45
  97.8 0.2 copy.22
  98.0 0.7 broadcast_in_dim.8
  98.7 4.3 %all-to-all-start = ((f32[8,4,1024]{2,1,0:T(4,128)}), f32[8,4,1024]{2,1,0:T(4,128)S(1)}, u32[]{:S(2)}, u32[]{:S(2)}) async-start(f32[8,4,1024]{2,1,0:T(4,128)} %broadcast_in_dim.8), calls=%async_computation | async-start | bytes 262144 | tf_op jit(solution)/shard_map/all_to_all | solution.py:75
  102.9 0.0 copy-done.1
  103.0 6.1 %all-to-all-done = f32[8,4,1024]{2,1,0:T(4,128)S(1)} async-done(((f32[8,4,1024]{2,1,0:T(4,128)}), f32[8,4,1024]{2,1,0:T(4,128)S(1)}, u32[]{:S(2)}, u32[]{:S(2)}) %all-to-all-start) | async-done | bytes 131104 | tf_op jit(solution)/shard_map/all_to_all | solution.py:75
  109.0 0.1 fusion.23
  109.3 0.8 fusion.21
  110.1 0.0 copy-done.3
  110.1 0.2 fusion.7
  110.3 12.7 %all_to_all.10 = f32[16,4,3]{1,2,0:T(4,128)S(1)} all-to-all(f32[16,4,3]{1,2,0:T(4,128)S(1)} %broadcast_in_dim.10), channel_id=1, replica_groups=mesh['dp'=16,'vocab'=8] {'dp'}, dimensions={0} | all-to-all | bytes 1536 | tf_op jit(solution)/shard_map/all_to_all | solution.py:97
  123.0 0.0 copy-done.2
  123.0 0.6 pad_maximum_fusion
  (14 shorter events, 0.1 us)
Async XLA Ops:
  7.2 5.1 %copy-start = (f32[1024]{0:T(1024)S(1)}, f32[1024]{0:T(1024)}, u32[]{:S(2)}) copy-start(f32[1024]{0:T(1024)} %param.8) | copy-start | bytes 12292
  7.2 76.4 %all-gather.2.cloned.1.call-start = ((), (), s32[]{:S(2)}) async-start(), calls=%async_computation.2 | async-start | bytes 8912896 | tf_op jit(solution)/shard_map/all_gather | solution.py:64
  83.6 19.4 %copy-start.1 = (s32[2]{0:T(128)S(1)}, s32[2]{0:T(128)}, u32[]{:S(2)}) copy-start(s32[2]{0:T(128)} %param.11) | copy-start | bytes 28
  83.6 26.5 %copy-start.3 = (s32[2,1]{0,1:T(1,128)S(1)}, s32[2,1]{0,1:T(1,128)}, u32[]{:S(2)}) copy-start(s32[2,1]{0,1:T(1,128)} %param.12) | copy-start | bytes 28
  83.6 39.4 %copy-start.2 = (f32[4]{0:T(128)S(1)}, f32[4]{0:T(128)}, u32[]{:S(2)}) copy-start(f32[4]{0:T(128)} %param.13) | copy-start | bytes 52
  98.7 10.4 %all-to-all-start = ((f32[8,4,1024]{2,1,0:T(4,128)}), f32[8,4,1024]{2,1,0:T(4,128)S(1)}, u32[]{:S(2)}, u32[]{:S(2)}) async-start(f32[8,4,1024]{2,1,0:T(4,128)} %broadcast_in_dim.8), calls=%async_computation | async-start | bytes 262144 | tf_op jit(solution)/shard_map/all_to_all | solution.py:75
Sparse Core Ops, SparseCore 0:
  10.1 73.4 all-gather.1

commit v6 on v5

--- a/solution.py
+++ b/solution.py
@@ -8,7 +8,7 @@
 from jax.sharding import PartitionSpec as P
 
 LANE = 128
-CHUNK = 512
+CHUNK = 256
 
 
 def stats_kernel(x_ref, w_ref, p_ref, o_ref, *, valid):

time: 131 us -> 130 us (level)
  no operation moved by 1% of the time
where the time goes in v6:
time: 130 us
  waiting for transfers between devices  75.3 us (58%)
  between operations  14.1 us (11%)
  Pallas kernels  13.8 us (11%)
  blocking collectives  12.7 us (10%)
  other arithmetic  6.52 us (5%)
  starting transfers between devices  4.29 us (3%)
  local copies, waits for them, and re-layouts  3.06 us (2%)
    all_gather x1, waiting for transfers between devices, per_device(): lax.all_gather(jnp.pad(head, ((0, 0), (0, padded - vocab_width))), 'dp',...  69.2 us
    pallas_call x1, Pallas kernels, row_stats(): pl.pallas_call(functools.partial(stats_kernel, valid=valid), grid=(1,), i...  13.8 us
    all_to_all x1, blocking collectives, per_device(): lax.all_to_all(partial_out, 'dp', 0, 0, tiled=False)  12.7 us
    all_to_all x1, waiting for transfers between devices, per_device(): gathered = lax.all_to_all(spread_out, 'vocab', 0, 0, tiled=False)  6.09 us
    all_to_all x1, starting transfers between devices, per_device(): gathered = lax.all_to_all(spread_out, 'vocab', 0, 0, tiled=False)  4.25 us
  transfers between devices with their start and end apart: 2, of which 2 were waited for; matrix products, arithmetic and copies ran while one was open for 4% of the time, Pallas kernels for 0%

profile of v6, /device:TPU:0, one launch (start us, length us, event | category | flops | bytes accessed | tf_op | source)
XLA Modules:
  0.0 130.0 jit_solution(9175454291026781356)
XLA Ops:
  7.2 0.0 copy-start
  7.2 0.0 all-gather.2.cloned.1.call-start
  7.2 1.9 %pad.4 = bf16[64,4096]{1,0:T(8,128)(2,1)} pad(bf16[64,4000]{1,0:T(8,128)(2,1)} %param.9, bf16[]{:T(256)} %constant.5.clone.1), padding=0_0x0_96 | pad | bytes 1036290 | tf_op jit(solution)/shard_map/jit(_pad)/pad | solution.py:64
  9.1 0.0 all-gather.2.cloned.1.call-update
  9.2 2.1 %multiply_reduce_fusion = f32[2,512]{1,0:T(2,128)S(1)} fusion(bf16[2,512,1024]{2,1,0:T(8,128)(2,1)} %param.7), kind=kLoop, calls=%fused_computation.3 | loop fusion | flops 3144704 | bytes 2101248 | tf_op jit(solution)/shard_map/reduce_sum | solution.py:67
  11.3 0.7 subtract_bitcast_fusion
  12.0 0.2 copy.38
  12.2 0.0 copy-done
  12.2 2.1 %fusion.1.x_ref = bf16[1024,1024]{1,0:T(8,128)(2,1)S(1)} fusion(f32[1024]{0:T(1024)S(1)} %copy-done, f32[1024]{0:T(1024)S(1)} %bitcast.51, bf16[2,512,1024]{2,1,0:T(8,128)(2,1)} %param.7), kind=kLoop, calls=%fused_computation.2 | loop fusion | flops 4194304 | bytes 4202496 | tf_op jit(solution)/shard_map/convert_element_type | solution.py:68
  14.4 69.2 %all-gather.2.cloned.1.call-done.w_ref = bf16[1024,4096]{1,0:T(8,128)(2,1)} async-done(((bf16[64,4096]{1,0:T(8,128)(2,1)}), bf16[1024,4096]{1,0:T(8,128)(2,1)}) %all-gather.2.cloned.1.call-update) | async-done | bytes 8388624 | tf_op jit(solution)/shard_map/all_gather | solution.py:64
  83.6 0.0 copy-start.1
  83.6 13.8 %shard_map.94 = f32[1024,4]{1,0:T(8,128)S(1)} custom-call(bf16[1024,1024]{1,0:T(8,128)(2,1)S(1)} %fusion.1.x_ref, bf16[1024,4096]{1,0:T(8,128)(2,1)} %all-gather.2.cloned.1.call-done.w_ref, s32[1024,1]{1,0:T(8,128)S(1)} %bitcast.48), custom_call_target="tpu_custom_call" | custom-call | tf_op jit(solution)/shard_map/pallas_call | solution.py:45
  97.4 0.2 copy.22
  97.6 0.7 broadcast_in_dim.8
  98.3 4.3 %all-to-all-start = ((f32[8,4,1024]{2,1,0:T(4,128)}), f32[8,4,1024]{2,1,0:T(4,128)S(1)}, u32[]{:S(2)}, u32[]{:S(2)}) async-start(f32[8,4,1024]{2,1,0:T(4,128)} %broadcast_in_dim.8), calls=%async_computation | async-start | bytes 262144 | tf_op jit(solution)/shard_map/all_to_all | solution.py:75
  102.5 0.0 copy-done.1
  102.6 6.1 %all-to-all-done = f32[8,4,1024]{2,1,0:T(4,128)S(1)} async-done(((f32[8,4,1024]{2,1,0:T(4,128)}), f32[8,4,1024]{2,1,0:T(4,128)S(1)}, u32[]{:S(2)}, u32[]{:S(2)}) %all-to-all-start) | async-done | bytes 131104 | tf_op jit(solution)/shard_map/all_to_all | solution.py:75
  108.6 0.1 fusion.23
  108.9 0.8 fusion.21
  109.7 0.0 copy-done.3
  109.7 0.2 fusion.7
  109.9 12.7 %all_to_all.10 = f32[16,4,3]{1,2,0:T(4,128)S(1)} all-to-all(f32[16,4,3]{1,2,0:T(4,128)S(1)} %broadcast_in_dim.10), channel_id=1, replica_groups=mesh['dp'=16,'vocab'=8] {'dp'}, dimensions={0} | all-to-all | bytes 1536 | tf_op jit(solution)/shard_map/all_to_all | solution.py:97
  122.6 0.0 copy-done.2
  122.6 0.6 pad_maximum_fusion
  (14 shorter events, 0.1 us)
Async XLA Ops:
  7.2 5.1 %copy-start = (f32[1024]{0:T(1024)S(1)}, f32[1024]{0:T(1024)}, u32[]{:S(2)}) copy-start(f32[1024]{0:T(1024)} %param.8) | copy-start | bytes 12292
  7.2 76.4 %all-gather.2.cloned.1.call-start = ((), (), s32[]{:S(2)}) async-start(), calls=%async_computation.2 | async-start | bytes 8912896 | tf_op jit(solution)/shard_map/all_gather | solution.py:64
  83.6 19.0 %copy-start.1 = (s32[2]{0:T(128)S(1)}, s32[2]{0:T(128)}, u32[]{:S(2)}) copy-start(s32[2]{0:T(128)} %param.11) | copy-start | bytes 28
  83.6 26.1 %copy-start.3 = (s32[2,1]{0,1:T(1,128)S(1)}, s32[2,1]{0,1:T(1,128)}, u32[]{:S(2)}) copy-start(s32[2,1]{0,1:T(1,128)} %param.12) | copy-start | bytes 28
  83.6 39.0 %copy-start.2 = (f32[4]{0:T(128)S(1)}, f32[4]{0:T(128)}, u32[]{:S(2)}) copy-start(f32[4]{0:T(128)} %param.13) | copy-start | bytes 52
  98.3 10.4 %all-to-all-start = ((f32[8,4,1024]{2,1,0:T(4,128)}), f32[8,4,1024]{2,1,0:T(4,128)S(1)}, u32[]{:S(2)}, u32[]{:S(2)}) async-start(f32[8,4,1024]{2,1,0:T(4,128)} %broadcast_in_dim.8), calls=%async_computation | async-start | bytes 262144 | tf_op jit(solution)/shard_map/all_to_all | solution.py:75
Sparse Core Ops, SparseCore 0:
  10.1 73.4 all-gather.1

commit v7 on v6

--- a/solution.py
+++ b/solution.py
@@ -93,8 +93,10 @@
     )
     partial_value = jnp.dot(member.T, seq_sums, precision=lax.Precision.HIGHEST)
     dp_count = lax.axis_size("dp")
-    partial_out = jnp.broadcast_to(partial_value[None], (dp_count,) + partial_value.shape)
-    group_value = jnp.sum(lax.all_to_all(partial_out, "dp", 0, 0, tiled=False), axis=0)
+    flat_value = partial_value.reshape(1, -1)
+    partial_out = jnp.broadcast_to(flat_value, (dp_count, flat_value.shape[1]))
+    summed = jnp.sum(lax.all_to_all(partial_out, "dp", 0, 0, tiled=True), axis=0)
+    group_value = summed.reshape(partial_value.shape)
     group_lp, group_ent, group_cnt = group_value[:, 0], group_value[:, 1], group_value[:, 2]
     shift = jnp.stack([group_lp / group_cnt - baseline, group_ent / group_cnt], axis=0)
     return (logprob, entropy, shift)

time: 130 us -> 131 us (level)
  no operation moved by 1% of the time
where the time goes in v7:
time: 131 us; the launch traced here: 130 us
  waiting for transfers between devices  75.3 us (57%)
  between operations  14.2 us (11%)
  Pallas kernels  13.8 us (11%)
  blocking collectives  12.7 us (10%)
  other arithmetic  6.73 us (5%)
  starting transfers between devices  4.29 us (3%)
  local copies, waits for them, and re-layouts  3.23 us (2%)
    all_gather x1, waiting for transfers between devices, per_device(): lax.all_gather(jnp.pad(head, ((0, 0), (0, padded - vocab_width))), 'dp',...  69.2 us
    pallas_call x1, Pallas kernels, row_stats(): pl.pallas_call(functools.partial(stats_kernel, valid=valid), grid=(1,), i...  13.8 us
    all_to_all x1, blocking collectives, per_device(): lax.all_to_all(partial_out, 'dp', 0, 0, tiled=True)  12.7 us
    all_to_all x1, waiting for transfers between devices, per_device(): gathered = lax.all_to_all(spread_out, 'vocab', 0, 0, tiled=False)  6.09 us
    all_to_all x1, starting transfers between devices, per_device(): gathered = lax.all_to_all(spread_out, 'vocab', 0, 0, tiled=False)  4.25 us
  transfers between devices with their start and end apart: 2, of which 2 were waited for; matrix products, arithmetic and copies ran while one was open for 4% of the time, Pallas kernels for 0%

profile of v7, /device:TPU:0, one launch (start us, length us, event | category | flops | bytes accessed | tf_op | source)
XLA Modules:
  0.0 130.5 jit_solution(12910448850428599096)
XLA Ops:
  7.2 0.0 copy-start
  7.2 0.0 all-gather.2.cloned.1.call-start
  7.2 1.9 %pad.4 = bf16[64,4096]{1,0:T(8,128)(2,1)} pad(bf16[64,4000]{1,0:T(8,128)(2,1)} %param.9, bf16[]{:T(256)} %constant.5.clone.1), padding=0_0x0_96 | pad | bytes 1036290 | tf_op jit(solution)/shard_map/jit(_pad)/pad | solution.py:64
  9.1 0.0 all-gather.2.cloned.1.call-update
  9.2 2.1 %multiply_reduce_fusion = f32[2,512]{1,0:T(2,128)S(1)} fusion(bf16[2,512,1024]{2,1,0:T(8,128)(2,1)} %param.7), kind=kLoop, calls=%fused_computation.3 | loop fusion | flops 3144704 | bytes 2101248 | tf_op jit(solution)/shard_map/reduce_sum | solution.py:67
  11.3 0.7 subtract_bitcast_fusion
  12.0 0.2 copy.45
  12.2 0.0 copy-done
  12.2 2.1 %fusion.1.x_ref = bf16[1024,1024]{1,0:T(8,128)(2,1)S(1)} fusion(f32[1024]{0:T(1024)S(1)} %copy-done, f32[1024]{0:T(1024)S(1)} %bitcast.46, bf16[2,512,1024]{2,1,0:T(8,128)(2,1)} %param.7), kind=kLoop, calls=%fused_computation.2 | loop fusion | flops 4194304 | bytes 4202496 | tf_op jit(solution)/shard_map/convert_element_type | solution.py:68
  14.4 69.2 %all-gather.2.cloned.1.call-done.w_ref = bf16[1024,4096]{1,0:T(8,128)(2,1)} async-done(((bf16[64,4096]{1,0:T(8,128)(2,1)}), bf16[1024,4096]{1,0:T(8,128)(2,1)}) %all-gather.2.cloned.1.call-update) | async-done | bytes 8388624 | tf_op jit(solution)/shard_map/all_gather | solution.py:64
  83.6 13.8 %shard_map.94 = f32[1024,4]{1,0:T(8,128)S(1)} custom-call(bf16[1024,1024]{1,0:T(8,128)(2,1)S(1)} %fusion.1.x_ref, bf16[1024,4096]{1,0:T(8,128)(2,1)} %all-gather.2.cloned.1.call-done.w_ref, s32[1024,1]{1,0:T(8,128)S(1)} %bitcast.43), custom_call_target="tpu_custom_call" | custom-call | tf_op jit(solution)/shard_map/pallas_call | solution.py:45
  97.4 0.2 copy.30
  97.6 0.7 broadcast_in_dim.10
  98.3 4.3 %all-to-all-start = ((f32[8,4,1024]{2,1,0:T(4,128)}), f32[8,4,1024]{2,1,0:T(4,128)S(1)}, u32[]{:S(2)}, u32[]{:S(2)}) async-start(f32[8,4,1024]{2,1,0:T(4,128)} %broadcast_in_dim.10), calls=%async_computation | async-start | bytes 262144 | tf_op jit(solution)/shard_map/all_to_all | solution.py:75
  102.5 0.0 copy-done.1
  102.6 6.1 %all-to-all-done = f32[8,4,1024]{2,1,0:T(4,128)S(1)} async-done(((f32[8,4,1024]{2,1,0:T(4,128)}), f32[8,4,1024]{2,1,0:T(4,128)S(1)}, u32[]{:S(2)}, u32[]{:S(2)}) %all-to-all-start) | async-done | bytes 131104 | tf_op jit(solution)/shard_map/all_to_all | solution.py:75
  108.6 0.1 fusion.21
  108.9 0.8 fusion.19
  109.7 0.3 fusion.7
  109.9 0.1 broadcast_in_dim.13
  110.0 12.7 %all_to_all.11 = f32[16,1,12]{2,1,0:T(1,128)S(1)} all-to-all(f32[16,1,12]{2,1,0:T(1,128)S(1)} %broadcast_in_dim.14), channel_id=1, replica_groups=mesh['dp'=16,'vocab'=8] {'dp'}, dimensions={0} | all-to-all | bytes 1536 | tf_op jit(solution)/shard_map/all_to_all | solution.py:98
  122.7 0.1 reshape.90
  122.8 0.2 fusion.13
  123.1 0.6 pad_maximum_fusion
  (16 shorter events, 0.1 us)
Async XLA Ops:
  7.2 5.1 %copy-start = (f32[1024]{0:T(1024)S(1)}, f32[1024]{0:T(1024)}, u32[]{:S(2)}) copy-start(f32[1024]{0:T(1024)} %param.8) | copy-start | bytes 12292
  7.2 76.4 %all-gather.2.cloned.1.call-start = ((), (), s32[]{:S(2)}) async-start(), calls=%async_computation.2 | async-start | bytes 8912896 | tf_op jit(solution)/shard_map/all_gather | solution.py:64
  83.6 19.0 %copy-start.1 = (s32[2]{0:T(128)S(1)}, s32[2]{0:T(128)}, u32[]{:S(2)}) copy-start(s32[2]{0:T(128)} %param.11) | copy-start | bytes 28
  83.6 26.1 %copy-start.2 = (s32[2,1]{0,1:T(1,128)S(1)}, s32[2,1]{0,1:T(1,128)}, u32[]{:S(2)}) copy-start(s32[2,1]{0,1:T(1,128)} %param.12) | copy-start | bytes 28
  83.6 39.5 %copy-start.3 = (f32[4]{0:T(128)S(1)}, f32[4]{0:T(128)}, u32[]{:S(2)}) copy-start(f32[4]{0:T(128)} %param.13) | copy-start | bytes 52
  98.3 10.4 %all-to-all-start = ((f32[8,4,1024]{2,1,0:T(4,128)}), f32[8,4,1024]{2,1,0:T(4,128)S(1)}, u32[]{:S(2)}, u32[]{:S(2)}) async-start(f32[8,4,1024]{2,1,0:T(4,128)} %broadcast_in_dim.10), calls=%async_computation | async-start | bytes 262144 | tf_op jit(solution)/shard_map/all_to_all | solution.py:75
Sparse Core Ops, SparseCore 0:
  10.1 73.4 all-gather.1

commit v8 on v5

--- a/solution.py
+++ b/solution.py
@@ -7,7 +7,6 @@
 from jax.experimental.pallas import tpu as pltpu
 from jax.sharding import PartitionSpec as P
 
-LANE = 128
 CHUNK = 512
 
 
@@ -17,30 +16,34 @@
     rows, width = x.shape[0], w_ref.shape[1]
     top = total = spread = chosen = None
     for k in range(width // CHUNK):
-        logits = jnp.dot(x, w_ref[:, k * CHUNK : (k + 1) * CHUNK], preferred_element_type=jnp.float32)
-        cols = lax.broadcasted_iota(jnp.int32, (rows, CHUNK), 1) + k * CHUNK
-        hit = jnp.sum(jnp.where(cols == picks, logits, 0.0), axis=1, keepdims=True)
+        logits = lax.dot_general(
+            w_ref[:, k * CHUNK : (k + 1) * CHUNK], x, (((0,), (1,)), ((), ())), preferred_element_type=jnp.float32
+        )
+        cols = lax.broadcasted_iota(jnp.int32, (CHUNK, rows), 0) + k * CHUNK
+        hit = jnp.sum(jnp.where(cols == picks, logits, 0.0), axis=0, keepdims=True)
         if (k + 1) * CHUNK > valid:
             logits = jnp.where(cols < valid, logits, -1e30)
-        chunk_top = jnp.max(logits, axis=1, keepdims=True)
+        chunk_top = jnp.max(logits, axis=0, keepdims=True)
         if top is None:
             shifted = logits - chunk_top
             expo = jnp.exp(shifted)
             top, chosen = chunk_top, hit
-            total = jnp.sum(expo, axis=1, keepdims=True)
-            spread = jnp.sum(expo * shifted, axis=1, keepdims=True)
+            total = jnp.sum(expo, axis=0, keepdims=True)
+            spread = jnp.sum(expo * shifted, axis=0, keepdims=True)
         else:
             new_top = jnp.maximum(top, chunk_top)
             factor = jnp.exp(top - new_top)
             shifted = logits - new_top
             expo = jnp.exp(shifted)
-            spread = factor * (spread + total * (top - new_top)) + jnp.sum(expo * shifted, axis=1, keepdims=True)
-            total = factor * total + jnp.sum(expo, axis=1, keepdims=True)
+            spread = factor * (spread + total * (top - new_top)) + jnp.sum(expo * shifted, axis=0, keepdims=True)
+            total = factor * total + jnp.sum(expo, axis=0, keepdims=True)
             top, chosen = new_top, chosen + hit
-    o_ref[...] = jnp.concatenate([top, total, spread, chosen], axis=1)
+    block = jnp.concatenate([top, total, spread, chosen], axis=0)
+    for peer in range(o_ref.shape[0]):
+        o_ref[peer] = block
 
 
-def row_stats(rows, weights, picks, valid):
+def row_stats(rows, weights, picks, valid, peers):
     count, width = rows.shape
     return pl.pallas_call(
         functools.partial(stats_kernel, valid=valid),
@@ -48,12 +51,12 @@
         in_specs=[
             pl.BlockSpec((count, width), lambda i: (0, 0)),
             pl.BlockSpec(weights.shape, lambda i: (0, 0)),
-            pl.BlockSpec((count, 1), lambda i: (0, 0)),
+            pl.BlockSpec((1, count), lambda i: (0, 0)),
         ],
-        out_specs=pl.BlockSpec((count, 4), lambda i: (0, 0)),
-        out_shape=jax.ShapeDtypeStruct((count, 4), jnp.float32),
+        out_specs=pl.BlockSpec((peers, 4, count), lambda i: (0, 0, 0)),
+        out_shape=jax.ShapeDtypeStruct((peers, 4, count), jnp.float32),
         compiler_params=pltpu.CompilerParams(vmem_limit_bytes=48 * 1024 * 1024),
-    )(rows, weights, picks.reshape(count, 1))
+    )(rows, weights, picks.reshape(1, count))
 
 
 def per_device(hidden, norm_gain, head, targets, lengths, groups, baseline):
@@ -69,9 +72,8 @@
     positions = jnp.arange(slot_count, dtype=jnp.int32)
     live = (positions[None, :] < lengths[:, None]).reshape(total_rows)
     wanted = targets.reshape(total_rows)
-    stats = row_stats(normed, weights, wanted - offset, vocab_width).T
     vocab_count = lax.axis_size("vocab")
-    spread_out = jnp.broadcast_to(stats[None], (vocab_count,) + stats.shape)
+    spread_out = row_stats(normed, weights, wanted - offset, vocab_width, vocab_count)
     gathered = lax.all_to_all(spread_out, "vocab", 0, 0, tiled=False)
     tops = gathered[:, 0]
     top = jnp.max(tops, axis=0)

time: 131 us -> 131 us (level)
  no operation moved by 1% of the time
where the time goes in v8:
time: 131 us
  waiting for transfers between devices  75.6 us (58%)
  Pallas kernels  15.3 us (12%)
  between operations  14.1 us (11%)
  blocking collectives  12.7 us (10%)
  other arithmetic  6.53 us (5%)
  starting transfers between devices  4.28 us (3%)
  local copies, waits for them, and re-layouts  1.97 us (2%)
    all_gather x1, waiting for transfers between devices, per_device(): lax.all_gather(jnp.pad(head, ((0, 0), (0, padded - vocab_width))), 'dp',...  69.5 us
    pallas_call x1, Pallas kernels, row_stats(): pl.pallas_call(functools.partial(stats_kernel, valid=valid), grid=(1,), i...  15.3 us
    all_to_all x1, blocking collectives, per_device(): lax.all_to_all(partial_out, 'dp', 0, 0, tiled=False)  12.7 us
    all_to_all x1, waiting for transfers between devices, per_device(): gathered = lax.all_to_all(spread_out, 'vocab', 0, 0, tiled=False)  6.09 us
    all_to_all x1, starting transfers between devices, per_device(): gathered = lax.all_to_all(spread_out, 'vocab', 0, 0, tiled=False)  4.25 us
  transfers between devices with their start and end apart: 2, of which 2 were waited for; matrix products, arithmetic and copies ran while one was open for 4% of the time, Pallas kernels for 0%

profile of v8, /device:TPU:0, one launch (start us, length us, event | category | flops | bytes accessed | tf_op | source)
XLA Modules:
  0.0 130.6 jit_solution(13369130560197273039)
XLA Ops:
  7.2 0.0 all-gather.2.cloned.1.call-start
  7.2 1.9 %pad.4 = bf16[64,4096]{1,0:T(8,128)(2,1)} pad(bf16[64,4000]{1,0:T(8,128)(2,1)} %param.9, bf16[]{:T(256)} %constant.5.clone.1), padding=0_0x0_96 | pad | bytes 1036290 | tf_op jit(solution)/shard_map/jit(_pad)/pad | solution.py:67
  9.1 0.0 all-gather.2.cloned.1.call-update
  9.2 0.7 subtract_bitcast_fusion
  9.9 2.1 %multiply_reduce_fusion = f32[2,512]{1,0:T(2,128)S(1)} fusion(bf16[2,512,1024]{2,1,0:T(8,128)(2,1)} %param.7), kind=kLoop, calls=%fused_computation.3 | loop fusion | flops 3144704 | bytes 2101248 | tf_op jit(solution)/shard_map/reduce_sum | solution.py:70
  12.0 2.2 %fusion.1.x_ref = bf16[1024,1024]{1,0:T(8,128)(2,1)S(1)} fusion(f32[1024]{0:T(1024)} %param.8, f32[1024]{0:T(1024)S(1)} %bitcast.47, bf16[2,512,1024]{2,1,0:T(8,128)(2,1)} %param.7), kind=kLoop, calls=%fused_computation.2 | loop fusion | flops 4194304 | bytes 4202496 | tf_op jit(solution)/shard_map/convert_element_type | solution.py:71
  14.1 69.5 %all-gather.2.cloned.1.call-done.w_ref = bf16[1024,4096]{1,0:T(8,128)(2,1)} async-done(((bf16[64,4096]{1,0:T(8,128)(2,1)}), bf16[1024,4096]{1,0:T(8,128)(2,1)}) %all-gather.2.cloned.1.call-update) | async-done | bytes 8388624 | tf_op jit(solution)/shard_map/all_gather | solution.py:67
  83.6 0.0 copy-start
  83.6 0.0 copy-start.2
  83.6 0.0 copy-start.1
  83.6 15.3 %shard_map.94 = f32[8,4,1024]{2,1,0:T(4,128)} custom-call(bf16[1024,1024]{1,0:T(8,128)(2,1)S(1)} %fusion.1.x_ref, bf16[1024,4096]{1,0:T(8,128)(2,1)} %all-gather.2.cloned.1.call-done.w_ref, s32[1,1024]{1,0:T(1,128)S(1)} %bitcast.46), custom_call_target="tpu_custom_call" | custom-call | tf_op jit(solution)/shard_map/pallas_call | solution.py:48
  98.9 4.2 %all-to-all-start = ((f32[8,4,1024]{2,1,0:T(4,128)}), f32[8,4,1024]{2,1,0:T(4,128)S(1)}, u32[]{:S(2)}, u32[]{:S(2)}) async-start(f32[8,4,1024]{2,1,0:T(4,128)} %shard_map.94), calls=%async_computation | async-start | bytes 262144 | tf_op jit(solution)/shard_map/all_to_all | solution.py:77
  103.1 0.0 copy-done
  103.1 6.1 %all-to-all-done = f32[8,4,1024]{2,1,0:T(4,128)S(1)} async-done(((f32[8,4,1024]{2,1,0:T(4,128)}), f32[8,4,1024]{2,1,0:T(4,128)S(1)}, u32[]{:S(2)}, u32[]{:S(2)}) %all-to-all-start) | async-done | bytes 131104 | tf_op jit(solution)/shard_map/all_to_all | solution.py:77
  109.2 0.1 fusion.23
  109.4 0.8 fusion.21
  110.2 0.0 copy-done.2
  110.2 0.2 fusion.7
  110.4 12.7 %all_to_all.10 = f32[16,4,3]{1,2,0:T(4,128)S(1)} all-to-all(f32[16,4,3]{1,2,0:T(4,128)S(1)} %broadcast_in_dim.8), channel_id=1, replica_groups=mesh['dp'=16,'vocab'=8] {'dp'}, dimensions={0} | all-to-all | bytes 1536 | tf_op jit(solution)/shard_map/all_to_all | solution.py:99
  123.2 0.0 copy-done.1
  123.2 0.6 pad_maximum_fusion
  (12 shorter events, 0.1 us)
Async XLA Ops:
  7.2 76.4 %all-gather.2.cloned.1.call-start = ((), (), s32[]{:S(2)}) async-start(), calls=%async_computation.2 | async-start | bytes 8912896 | tf_op jit(solution)/shard_map/all_gather | solution.py:67
  83.6 19.5 %copy-start = (s32[2]{0:T(128)S(1)}, s32[2]{0:T(128)}, u32[]{:S(2)}) copy-start(s32[2]{0:T(128)} %param.11) | copy-start | bytes 28
  83.6 26.6 %copy-start.2 = (s32[2,1]{0,1:T(1,128)S(1)}, s32[2,1]{0,1:T(1,128)}, u32[]{:S(2)}) copy-start(s32[2,1]{0,1:T(1,128)} %param.12) | copy-start | bytes 28
  83.6 39.6 %copy-start.1 = (f32[4]{0:T(128)S(1)}, f32[4]{0:T(128)}, u32[]{:S(2)}) copy-start(f32[4]{0:T(128)} %param.13) | copy-start | bytes 52
  98.9 10.3 %all-to-all-start = ((f32[8,4,1024]{2,1,0:T(4,128)}), f32[8,4,1024]{2,1,0:T(4,128)S(1)}, u32[]{:S(2)}, u32[]{:S(2)}) async-start(f32[8,4,1024]{2,1,0:T(4,128)} %shard_map.94), calls=%async_computation | async-start | bytes 262144 | tf_op jit(solution)/shard_map/all_to_all | solution.py:77
Sparse Core Ops, SparseCore 0:
  10.1 73.4 all-gather.1
